TPU v7x, 32 devices: a whole 2x2x4 slice. The times are simulated.
32 devices in a mesh: lon: 16 (over z, y, core), lat: 2 (over x).
Axes of the slice: x: 2, y: 2, z: 4, core: 2. Of those that a mesh axis runs over, the one named last changes fastest.
Arguments:
- field: float32 [2, 512, 512], P(None, 'lon', 'lat'), may hold values from -6 to 6
- offsets: int32 [512], P('lat'), may hold values from 0 to 511, as said below
- fraction: float32 [512], P('lat'), may hold values from 0 to 1
- helm: float32 [2], replicated, may hold values from 4 to 32
Outputs:
- solution: float32 [2, 512, 512], P(None, 'lon', 'lat')
Inputs may be any that keep to these rules, and one draw needn't show every extreme that they name: `offsets`: each row's offset is a whole number of longitude points; some row needs the whole circle but one point, some row none.
All inputs are finite; a program needn't handle non-finite values.
Results may differ from a plain program's by a relative error of at most 0.00002.
Values sent between devices are 32-bit elements; how exact they have to be, the bound alone decides.
No kernel may reach another device: no remote copies, remote signals or barrier semaphores. Data moves between devices by JAX's collectives and lax.ppermute only.
A program may use at most 64 MiB of HBM per device.

v0:
```python
import jax
import jax.numpy as jnp
from jax import lax
from jax.sharding import PartitionSpec as P

SMOOTH = 2
COARSE = 4


OMEGA = 0.8


def with_halo(cells, sides, width, closed):
    for axis, dim in sides:
        count = lax.axis_size(axis)
        ends = count if closed else count - 1
        head = lax.slice_in_dim(cells, 0, width, axis=dim)
        tail = lax.slice_in_dim(cells, cells.shape[dim] - width, cells.shape[dim], axis=dim)
        cells = jnp.concatenate(
            [
                lax.ppermute(tail, axis, [(i, (i + 1) % count) for i in range(ends)]),
                cells,
                lax.ppermute(head, axis, [((i + 1) % count, i) for i in range(ends)]),
            ],
            axis=dim,
        )
    return cells


def passed_along(shard, axis, by):
    count = lax.axis_size(axis)
    return lax.ppermute(shard, axis, [(i, (i + by) % count) for i in range(count)])


def zonal_pair(x):
    rim = with_halo(x, (("lon", 1),), 1, True)
    return rim[:, 2:, :] + rim[:, :-2, :]


def meridional_pair(x):
    rim = with_halo(x, (("lat", 2),), 1, False)
    return rim[:, :, 2:] + rim[:, :, :-2]


def padded_pair(x):
    padded = jnp.pad(x, ((0, 0), (0, 0), (1, 1)))
    return padded[:, :, 2:] + padded[:, :, :-2]


def relax(x, rhs, coef, pair):
    diag = 1.0 + 4.0 * coef
    applied = diag * x - coef * (zonal_pair(x) + pair(x))
    return x + OMEGA * (rhs - applied) / diag


def defect(x, rhs, coef, pair):
    diag = 1.0 + 4.0 * coef
    return rhs - (diag * x - coef * (zonal_pair(x) + pair(x)))


def restrict(x):
    lev, nlon, nlat = x.shape
    return x.reshape(lev, nlon // 2, 2, nlat // 2, 2).mean(axis=(2, 4))


def prolong(x):
    return jnp.repeat(jnp.repeat(x, 2, axis=1), 2, axis=2)


def per_device(field, offsets, fraction, helm):
    width = field.shape[1]
    circuit = lax.axis_size("lon")
    block_shift = offsets // width
    remain = offsets % width
    moved = field
    for bit in range((circuit - 1).bit_length()):
        hopped = passed_along(moved, "lon", 1 << bit)
        take = block_shift // (1 << bit) % 2 == 1
        moved = jnp.where(take[None, None, :], hopped, moved)
    before = passed_along(moved, "lon", 1)
    current = jnp.concatenate([before, moved], axis=1)
    for bit in range((width - 1).bit_length()):
        rolled = jnp.roll(current, 1 << bit, axis=1)
        pick = remain // (1 << bit) % 2 == 1
        current = jnp.where(pick[None, None, :], rolled, current)
    shifted = current[:, width:, :]
    rim = with_halo(shifted, (("lon", 1),), 2, True)
    s = fraction[None, None, :]
    w_one = -s * (s - 1.0) * (s - 2.0) / 6.0
    w_two = (s + 1.0) * (s - 1.0) * (s - 2.0) / 2.0
    w_three = -(s + 1.0) * s * (s - 2.0) / 2.0
    w_four = (s + 1.0) * s * (s - 1.0) / 6.0
    departure = (
        w_one * rim[:, 3 : width + 3]
        + w_two * rim[:, 2 : width + 2]
        + w_three * rim[:, 1 : width + 1]
        + w_four * rim[:, 0:width]
    )
    coef0 = helm[:, None, None]
    coef1 = coef0 / 4.0
    coef2 = coef0 / 16.0
    level0 = jnp.zeros_like(departure)
    for sweep in range(SMOOTH):
        level0 = relax(level0, departure, coef0, meridional_pair)
    rhs1 = restrict(defect(level0, departure, coef0, meridional_pair))
    level1 = jnp.zeros_like(rhs1)
    for sweep in range(SMOOTH):
        level1 = relax(level1, rhs1, coef1, meridional_pair)
    rhs2 = restrict(defect(level1, rhs1, coef1, meridional_pair))
    coarse_rows_dev = rhs2.shape[2]
    whole = lax.all_gather(rhs2, "lat", axis=2, tiled=True)
    level2 = jnp.zeros_like(whole)
    for sweep in range(COARSE):
        level2 = relax(level2, whole, coef2, padded_pair)
    level2 = lax.dynamic_slice_in_dim(
        level2, lax.axis_index("lat") * coarse_rows_dev, coarse_rows_dev, 2
    )
    level1 = level1 + prolong(level2)
    for sweep in range(SMOOTH):
        level1 = relax(level1, rhs1, coef1, meridional_pair)
    level0 = level0 + prolong(level1)
    for sweep in range(SMOOTH):
        level0 = relax(level0, departure, coef0, meridional_pair)
    return level0


def solution(mesh):
    return jax.shard_map(
        per_device,
        mesh=mesh,
        in_specs=(P(None, "lon", "lat"), P("lat"), P("lat"), P()),
        out_specs=P(None, "lon", "lat"),
        check_vma=False,
    )
```

profile of v0, /device:TPU:0, one launch (start us, length us, event | category | flops | bytes accessed | tf_op | source)
XLA Modules:
  0.0 190.6 jit_solution(4597889950592666039)
XLA Ops:
  2.2 8.3 %collective-permute-done = f32[2,32,256]{1,2,0:T(8,128)S(1)} collective-permute-done((f32[2,32,256]{1,2,0:T(8,128)S(1)}, f32[2,32,256]{1,2,0:T(8,128)S(1)}, u32[]{:S(2)}, u32[]{:S(2)}) %collective-permute-start) | collective-permute-done | bytes 65568 | tf_op jit(solution)/shard_map/ppermute | solution.py:32
  10.7 10.0 %collective-permute-done.1 = f32[2,32,256]{1,2,0:T(8,128)S(1)} collective-permute-done((f32[2,32,256]{1,2,0:T(8,128)S(1)}, f32[2,32,256]{1,2,0:T(8,128)S(1)}, u32[]{:S(2)}, u32[]{:S(2)}) %collective-permute-start.1) | collective-permute-done | bytes 65568 | tf_op jit(solution)/shard_map/ppermute | solution.py:32
  21.5 4.8 %collective-permute-start.10 = (f32[2,32,1]{1,2,0:T(1,128)S(1)}, f32[2,32,1]{1,2,0:T(1,128)S(1)}, u32[]{:S(2)}, u32[]{:S(2)}) collective-permute-start(f32[2,32,1]{1,2,0:T(1,128)S(1)} %broadcast.224), channel_id=1, source_target_pairs={{0,1},{2,3},{4,5},{6,7},{8,9},{10,11},{12,13},{14,15},{16,17},{18,... | collective-permute-start | bytes 776 | tf_op jit(solution)/shard_map/ppermute | solution.py:21
  26.3 1.3 collective-permute-start.9
  27.6 1.5 collective-permute-done.2
  29.9 12.3 %collective-permute-done.3 = f32[2,32,256]{1,2,0:T(8,128)S(1)} collective-permute-done((f32[2,32,256]{1,2,0:T(8,128)S(1)}, f32[2,32,256]{1,2,0:T(8,128)S(1)}, u32[]{:S(2)}, u32[]{:S(2)}) %collective-permute-start.3) | collective-permute-done | bytes 65568 | tf_op jit(solution)/shard_map/ppermute | solution.py:32
  42.5 8.3 %collective-permute-done.4 = f32[2,32,256]{1,2,0:T(8,128)S(1)} collective-permute-done((f32[2,32,256]{1,2,0:T(8,128)S(1)}, f32[2,32,256]{1,2,0:T(8,128)S(1)}, u32[]{:S(2)}, u32[]{:S(2)}) %collective-permute-start.4) | collective-permute-done | bytes 65568 | tf_op jit(solution)/shard_map/ppermute | solution.py:32
  53.4 3.2 %collective-permute-done.5 = f32[2,2,256]{1,2,0:T(8,128)S(1)} collective-permute-done((f32[2,2,256]{1,2,0:T(8,128)S(1)}, f32[2,2,256]{1,2,0:T(8,128)S(1)}, u32[]{:S(2)}, u32[]{:S(2)}) %collective-permute-start.5) | collective-permute-done | bytes 4128 | tf_op jit(solution)/shard_map/ppermute | solution.py:23
  56.7 4.7 %collective-permute-done.6 = f32[2,2,256]{1,2,0:T(8,128)S(1)} collective-permute-done((f32[2,2,256]{1,2,0:T(8,128)S(1)}, f32[2,2,256]{1,2,0:T(8,128)S(1)}, u32[]{:S(2)}, u32[]{:S(2)}) %collective-permute-start.6) | collective-permute-done | bytes 4128 | tf_op jit(solution)/shard_map/ppermute | solution.py:21
  62.7 1.3 collective-permute-start.13
  63.9 4.5 %collective-permute-start.14 = (f32[2,32,1]{1,2,0:T(1,128)S(1)}, f32[2,32,1]{1,2,0:T(1,128)S(1)}, u32[]{:S(2)}, u32[]{:S(2)}) collective-permute-start(f32[2,32,1]{1,2,0:T(1,128)S(1)} %get-tuple-element.27), channel_id=1, source_target_pairs={{0,1},{2,3},{4,5},{6,7},{8,9},{10,11},{12,13},{14,15},{16,17},{18,... | collective-permute-start | bytes 776 | tf_op jit(solution)/shard_map/ppermute | solution.py:21
  68.5 1.3 collective-permute-done.14
  71.1 2.0 %collective-permute-start.15 = (f32[2,1,256]{1,2,0:T(8,128)S(1)}, f32[2,1,256]{1,2,0:T(8,128)S(1)}, u32[]{:S(2)}, u32[]{:S(2)}) collective-permute-start(f32[2,1,256]{1,2,0:T(8,128)S(1)} %get-tuple-element.20), channel_id=1, source_target_pairs={{2,0},{4,2},{6,4},{8,6},{10,8},{12,10},{14,12},{16,14},{18,16},{20... | collective-permute-start | bytes 6152 | tf_op jit(solution)/shard_map/ppermute | solution.py:23
  73.1 1.3 collective-permute-start.17
  74.4 4.5 %collective-permute-start.18 = (f32[2,32,1]{1,2,0:T(1,128)S(1)}, f32[2,32,1]{1,2,0:T(1,128)S(1)}, u32[]{:S(2)}, u32[]{:S(2)}) collective-permute-start(f32[2,32,1]{1,2,0:T(1,128)S(1)} %get-tuple-element.23), channel_id=1, source_target_pairs={{0,1},{2,3},{4,5},{6,7},{8,9},{10,11},{12,13},{14,15},{16,17},{18,... | collective-permute-start | bytes 776 | tf_op jit(solution)/shard_map/ppermute | solution.py:21
  79.0 3.9 %collective-permute-start.19 = (f32[2,1,128]{2,1,0:T(1,128)S(1)}, f32[2,1,128]{2,1,0:T(1,128)S(1)}, u32[]{:S(2)}, u32[]{:S(2)}) collective-permute-start(f32[2,1,128]{2,1,0:T(1,128)S(1)} %broadcast.227), channel_id=1, source_target_pairs={{2,0},{4,2},{6,4},{8,6},{10,8},{12,10},{14,12},{16,14},{18,16},{20... | collective-permute-start | bytes 3080 | tf_op jit(solution)/shard_map/ppermute | solution.py:23
  82.9 1.3 collective-permute-start.21
  84.2 4.5 %collective-permute-start.22 = (f32[2,16,1]{2,1,0:T(8,128)S(1)}, f32[2,16,1]{2,1,0:T(8,128)S(1)}, u32[]{:S(2)}, u32[]{:S(2)}) collective-permute-start(f32[2,16,1]{2,1,0:T(8,128)S(1)} %broadcast.228), channel_id=1, source_target_pairs={{0,1},{2,3},{4,5},{6,7},{8,9},{10,11},{12,13},{14,15},{16,17},{18,... | collective-permute-start | bytes 392 | tf_op jit(solution)/shard_map/ppermute | solution.py:21
  89.2 5.5 %reshape.62 = f32[2,16,2,128,2]{4,3,2,1,0:T(8,128)} reshape(f32[2,32,256]{2,1,0:T(8,128)S(1)} %copy.234) | data formatting | bytes 131072 | tf_op jit(solution)/shard_map/reshape | solution.py:63
  94.7 2.8 %reduce_sum.18 = f32[2,16,128]{2,1,0:T(8,128)S(1)} reduce(f32[2,16,2,128,2]{4,3,2,1,0:T(8,128)} %reshape.62, f32[]{:T(128)} %constant.199.clone.1), dimensions={2,4}, to_apply=%region_0.1 | reduce | flops 12288 | bytes 81924 | tf_op jit(solution)/shard_map/reduce_sum | solution.py:63
  97.7 3.9 %collective-permute-start.23 = (f32[2,1,128]{2,1,0:T(1,128)S(1)}, f32[2,1,128]{2,1,0:T(1,128)S(1)}, u32[]{:S(2)}, u32[]{:S(2)}) collective-permute-start(f32[2,1,128]{2,1,0:T(1,128)S(1)} %get-tuple-element.42), channel_id=1, source_target_pairs={{2,0},{4,2},{6,4},{8,6},{10,8},{12,10},{14,12},{16,14},{18,16},{20... | collective-permute-start | bytes 3080 | tf_op jit(solution)/shard_map/ppermute | solution.py:23
  101.7 1.3 collective-permute-start.25
  102.9 4.5 %collective-permute-start.26 = (f32[2,16,1]{2,1,0:T(8,128)S(1)}, f32[2,16,1]{2,1,0:T(8,128)S(1)}, u32[]{:S(2)}, u32[]{:S(2)}) collective-permute-start(f32[2,16,1]{2,1,0:T(8,128)S(1)} %get-tuple-element.45), channel_id=1, source_target_pairs={{0,1},{2,3},{4,5},{6,7},{8,9},{10,11},{12,13},{14,15},{16,17},{18,... | collective-permute-start | bytes 392 | tf_op jit(solution)/shard_map/ppermute | solution.py:21
  107.5 1.4 collective-permute-done.26
  109.1 1.3 collective-permute-start.29
  110.4 4.5 %collective-permute-start.30 = (f32[2,16,1]{2,1,0:T(8,128)S(1)}, f32[2,16,1]{2,1,0:T(8,128)S(1)}, u32[]{:S(2)}, u32[]{:S(2)}) collective-permute-start(f32[2,16,1]{2,1,0:T(8,128)S(1)} %get-tuple-element.41), channel_id=1, source_target_pairs={{0,1},{2,3},{4,5},{6,7},{8,9},{10,11},{12,13},{14,15},{16,17},{18,... | collective-permute-start | bytes 392 | tf_op jit(solution)/shard_map/ppermute | solution.py:21
  114.9 2.8 %collective-permute-start.27 = (f32[2,1,128]{2,1,0:T(1,128)S(1)}, f32[2,1,128]{2,1,0:T(1,128)S(1)}, u32[]{:S(2)}, u32[]{:S(2)}) collective-permute-start(f32[2,1,128]{2,1,0:T(1,128)S(1)} %get-tuple-element.38), channel_id=1, source_target_pairs={{2,0},{4,2},{6,4},{8,6},{10,8},{12,10},{14,12},{16,14},{18,16},{20... | collective-permute-start | bytes 3080 | tf_op jit(solution)/shard_map/ppermute | solution.py:23
  119.0 4.4 %collective-permute-done.28 = f32[2,1,128]{2,1,0:T(1,128)S(1)} collective-permute-done((f32[2,1,128]{2,1,0:T(1,128)S(1)}, f32[2,1,128]{2,1,0:T(1,128)S(1)}, u32[]{:S(2)}, u32[]{:S(2)}) %collective-permute-start.28) | collective-permute-done | bytes 1056 | tf_op jit(solution)/shard_map/ppermute | solution.py:21
  124.9 4.9 %all_gather.3 = f32[2,8,128]{1,0,2:T(2,128)S(1)} all-gather(f32[2,8,64]{1,0,2:T(2,128)S(1)} %copy.235), channel_id=1, replica_groups=mesh['lon'=16,'lat'=2] {'lat'}, dimensions={2}, use_global_device_ids=true | all-gather | bytes 12288 | tf_op jit(solution)/shard_map/all_gather | solution.py:111
  131.3 4.5 %collective-permute-done.32 = f32[2,1,128]{2,1,0:T(1,128)S(1)} collective-permute-done((f32[2,1,128]{2,1,0:T(1,128)S(1)}, f32[2,1,128]{2,1,0:T(1,128)S(1)}, u32[]{:S(2)}, u32[]{:S(2)}) %collective-permute-start.32) | collective-permute-done | bytes 1056 | tf_op jit(solution)/shard_map/ppermute | solution.py:21
  137.2 4.5 %collective-permute-done.34 = f32[2,1,128]{2,1,0:T(1,128)S(1)} collective-permute-done((f32[2,1,128]{2,1,0:T(1,128)S(1)}, f32[2,1,128]{2,1,0:T(1,128)S(1)}, u32[]{:S(2)}, u32[]{:S(2)}) %collective-permute-start.34) | collective-permute-done | bytes 1056 | tf_op jit(solution)/shard_map/ppermute | solution.py:21
  143.1 4.5 %collective-permute-done.36 = f32[2,1,128]{2,1,0:T(1,128)S(1)} collective-permute-done((f32[2,1,128]{2,1,0:T(1,128)S(1)}, f32[2,1,128]{2,1,0:T(1,128)S(1)}, u32[]{:S(2)}, u32[]{:S(2)}) %collective-permute-start.36) | collective-permute-done | bytes 1056 | tf_op jit(solution)/shard_map/ppermute | solution.py:21
  148.6 1.3 collective-permute-start.39
  149.9 4.5 %collective-permute-start.40 = (f32[2,16,1]{2,1,0:T(8,128)S(1)}, f32[2,16,1]{2,1,0:T(8,128)S(1)}, u32[]{:S(2)}, u32[]{:S(2)}) collective-permute-start(f32[2,16,1]{2,1,0:T(8,128)S(1)} %get-tuple-element.37), channel_id=1, source_target_pairs={{0,1},{2,3},{4,5},{6,7},{8,9},{10,11},{12,13},{14,15},{16,17},{18,... | collective-permute-start | bytes 392 | tf_op jit(solution)/shard_map/ppermute | solution.py:21
  154.5 1.4 collective-permute-done.40
  156.0 2.9 %collective-permute-start.41 = (f32[2,1,128]{2,1,0:T(1,128)S(1)}, f32[2,1,128]{2,1,0:T(1,128)S(1)}, u32[]{:S(2)}, u32[]{:S(2)}) collective-permute-start(f32[2,1,128]{2,1,0:T(1,128)S(1)} %get-tuple-element.30), channel_id=1, source_target_pairs={{2,0},{4,2},{6,4},{8,6},{10,8},{12,10},{14,12},{16,14},{18,16},{20... | collective-permute-start | bytes 3080 | tf_op jit(solution)/shard_map/ppermute | solution.py:23
  159.0 1.3 collective-permute-start.43
  160.3 4.5 %collective-permute-start.44 = (f32[2,16,1]{2,1,0:T(8,128)S(1)}, f32[2,16,1]{2,1,0:T(8,128)S(1)}, u32[]{:S(2)}, u32[]{:S(2)}) collective-permute-start(f32[2,16,1]{2,1,0:T(8,128)S(1)} %get-tuple-element.33), channel_id=1, source_target_pairs={{0,1},{2,3},{4,5},{6,7},{8,9},{10,11},{12,13},{14,15},{16,17},{18,... | collective-permute-start | bytes 392 | tf_op jit(solution)/shard_map/ppermute | solution.py:21
  164.9 1.4 collective-permute-done.44
  166.8 3.4 %collective-permute-start.45 = (f32[2,1,256]{1,2,0:T(8,128)S(1)}, f32[2,1,256]{1,2,0:T(8,128)S(1)}, u32[]{:S(2)}, u32[]{:S(2)}) collective-permute-start(f32[2,1,256]{1,2,0:T(8,128)S(1)} %get-tuple-element.16), channel_id=1, source_target_pairs={{2,0},{4,2},{6,4},{8,6},{10,8},{12,10},{14,12},{16,14},{18,16},{20... | collective-permute-start | bytes 6152 | tf_op jit(solution)/shard_map/ppermute | solution.py:23
  170.1 1.3 collective-permute-start.47
  171.4 4.5 %collective-permute-start.48 = (f32[2,32,1]{1,2,0:T(1,128)S(1)}, f32[2,32,1]{1,2,0:T(1,128)S(1)}, u32[]{:S(2)}, u32[]{:S(2)}) collective-permute-start(f32[2,32,1]{1,2,0:T(1,128)S(1)} %get-tuple-element.19), channel_id=1, source_target_pairs={{0,1},{2,3},{4,5},{6,7},{8,9},{10,11},{12,13},{14,15},{16,17},{18,... | collective-permute-start | bytes 776 | tf_op jit(solution)/shard_map/ppermute | solution.py:21
  177.3 1.5 collective-permute-done.46
  179.2 1.9 collective-permute-start.49
  181.1 1.3 collective-permute-start.51
  182.4 4.5 %collective-permute-start.52 = (f32[2,32,1]{1,2,0:T(1,128)S(1)}, f32[2,32,1]{1,2,0:T(1,128)S(1)}, u32[]{:S(2)}, u32[]{:S(2)}) collective-permute-start(f32[2,32,1]{1,2,0:T(1,128)S(1)} %get-tuple-element.15), channel_id=1, source_target_pairs={{0,1},{2,3},{4,5},{6,7},{8,9},{10,11},{12,13},{14,15},{16,17},{18,... | collective-permute-start | bytes 776 | tf_op jit(solution)/shard_map/ppermute | solution.py:21
  186.9 1.3 collective-permute-done.52
  188.2 1.4 collective-permute-done.50
  (142 shorter events, 21.6 us)
Async XLA Ops:
  1.0 9.6 %collective-permute-start = (f32[2,32,256]{1,2,0:T(8,128)S(1)}, f32[2,32,256]{1,2,0:T(8,128)S(1)}, u32[]{:S(2)}, u32[]{:S(2)}) collective-permute-start(f32[2,32,256]{1,2,0:T(8,128)S(1)} %copy.232), channel_id=1, source_target_pairs={{0,2},{2,4},{4,6},{6,8},{8,10},{10,12},{12,14},{14,16},{16,18},{18... | collective-permute-start | bytes 196616 | tf_op jit(solution)/shard_map/ppermute | solution.py:32
  10.7 10.0 %collective-permute-start.1 = (f32[2,32,256]{1,2,0:T(8,128)S(1)}, f32[2,32,256]{1,2,0:T(8,128)S(1)}, u32[]{:S(2)}, u32[]{:S(2)}) collective-permute-start(f32[2,32,256]{1,2,0:T(8,128)S(1)} %broadcast_select_fusion), channel_id=1, source_target_pairs={{0,4},{2,6},{4,8},{6,10},{8,12},{10,14},{12,16},{14,18},{16,20},{1... | collective-permute-start | bytes 196616 | tf_op jit(solution)/shard_map/ppermute | solution.py:32
  20.8 8.2 %collective-permute-start.2 = (f32[2,32,256]{1,2,0:T(8,128)S(1)}, f32[2,32,256]{1,2,0:T(8,128)S(1)}, u32[]{:S(2)}, u32[]{:S(2)}) collective-permute-start(f32[2,32,256]{1,2,0:T(8,128)S(1)} %broadcast_select_fusion.1), channel_id=1, source_target_pairs={{0,8},{2,10},{4,12},{6,14},{8,16},{10,18},{12,20},{14,22},{16,24},... | collective-permute-start | bytes 196616 | tf_op jit(solution)/shard_map/ppermute | solution.py:32
  20.9 32.5 %collective-permute-start.7 = (f32[2,1,256]{1,2,0:T(8,128)S(1)}, f32[2,1,256]{1,2,0:T(8,128)S(1)}, u32[]{:S(2)}, u32[]{:S(2)}) collective-permute-start(f32[2,1,256]{1,2,0:T(8,128)S(1)} %broadcast.223), channel_id=1, source_target_pairs={{2,0},{4,2},{6,4},{8,6},{10,8},{12,10},{14,12},{16,14},{18,16},{20... | collective-permute-start | bytes 6152 | tf_op jit(solution)/shard_map/ppermute | solution.py:23
  21.0 32.5 %collective-permute-start.8 = (f32[2,1,256]{1,2,0:T(8,128)S(1)}, f32[2,1,256]{1,2,0:T(8,128)S(1)}, u32[]{:S(2)}, u32[]{:S(2)}) collective-permute-start(f32[2,1,256]{1,2,0:T(8,128)S(1)} %broadcast.223), channel_id=1, source_target_pairs={{0,2},{2,4},{4,6},{6,8},{8,10},{10,12},{12,14},{14,16},{16,18},{18... | collective-permute-start | bytes 6152 | tf_op jit(solution)/shard_map/ppermute | solution.py:21
  21.5 31.3 %collective-permute-start.10 = (f32[2,32,1]{1,2,0:T(1,128)S(1)}, f32[2,32,1]{1,2,0:T(1,128)S(1)}, u32[]{:S(2)}, u32[]{:S(2)}) collective-permute-start(f32[2,32,1]{1,2,0:T(1,128)S(1)} %broadcast.224), channel_id=1, source_target_pairs={{0,1},{2,3},{4,5},{6,7},{8,9},{10,11},{12,13},{14,15},{16,17},{18,... | collective-permute-start | bytes 776 | tf_op jit(solution)/shard_map/ppermute | solution.py:21
  26.3 27.1 %collective-permute-start.9 = (f32[2,32,1]{1,2,0:T(1,128)S(1)}, f32[2,32,1]{1,2,0:T(1,128)S(1)}, u32[]{:S(2)}, u32[]{:S(2)}) collective-permute-start(f32[2,32,1]{1,2,0:T(1,128)S(1)} %broadcast.224), channel_id=1, source_target_pairs={{1,0},{3,2},{5,4},{7,6},{9,8},{11,10},{13,12},{15,14},{17,16},{19,... | collective-permute-start | bytes 776 | tf_op jit(solution)/shard_map/ppermute | solution.py:23
  29.1 13.1 %collective-permute-start.3 = (f32[2,32,256]{1,2,0:T(8,128)S(1)}, f32[2,32,256]{1,2,0:T(8,128)S(1)}, u32[]{:S(2)}, u32[]{:S(2)}) collective-permute-start(f32[2,32,256]{1,2,0:T(8,128)S(1)} %broadcast_select_fusion.2), channel_id=1, source_target_pairs={{0,16},{2,18},{4,20},{6,22},{8,24},{10,26},{12,28},{14,30},{16,0},... | collective-permute-start | bytes 196616 | tf_op jit(solution)/shard_map/ppermute | solution.py:32
  42.3 8.5 %collective-permute-start.4 = (f32[2,32,256]{1,2,0:T(8,128)S(1)}, f32[2,32,256]{1,2,0:T(8,128)S(1)}, u32[]{:S(2)}, u32[]{:S(2)}) collective-permute-start(f32[2,32,256]{1,2,0:T(8,128)S(1)} %broadcast_select_fusion.3), channel_id=1, source_target_pairs={{0,2},{2,4},{4,6},{6,8},{8,10},{10,12},{12,14},{14,16},{16,18},{18... | collective-permute-start | bytes 196616 | tf_op jit(solution)/shard_map/ppermute | solution.py:32
  52.8 8.5 %collective-permute-start.6 = (f32[2,2,256]{1,2,0:T(8,128)S(1)}, f32[2,2,256]{1,2,0:T(8,128)S(1)}, u32[]{:S(2)}, u32[]{:S(2)}) collective-permute-start(f32[2,2,256]{1,2,0:T(8,128)S(1)} %get-tuple-element.29), channel_id=1, source_target_pairs={{0,2},{2,4},{4,6},{6,8},{8,10},{10,12},{12,14},{14,16},{16,18},{18... | collective-permute-start | bytes 12296 | tf_op jit(solution)/shard_map/ppermute | solution.py:21
  62.1 7.7 %collective-permute-start.11 = (f32[2,1,256]{1,2,0:T(8,128)S(1)}, f32[2,1,256]{1,2,0:T(8,128)S(1)}, u32[]{:S(2)}, u32[]{:S(2)}) collective-permute-start(f32[2,1,256]{1,2,0:T(8,128)S(1)} %get-tuple-element.24), channel_id=1, source_target_pairs={{2,0},{4,2},{6,4},{8,6},{10,8},{12,10},{14,12},{16,14},{18,16},{20... | collective-permute-start | bytes 6152 | tf_op jit(solution)/shard_map/ppermute | solution.py:23
  62.2 8.5 %collective-permute-start.12 = (f32[2,1,256]{1,2,0:T(8,128)S(1)}, f32[2,1,256]{1,2,0:T(8,128)S(1)}, u32[]{:S(2)}, u32[]{:S(2)}) collective-permute-start(f32[2,1,256]{1,2,0:T(8,128)S(1)} %get-tuple-element.25), channel_id=1, source_target_pairs={{0,2},{2,4},{4,6},{6,8},{8,10},{10,12},{12,14},{14,16},{16,18},{18... | collective-permute-start | bytes 6152 | tf_op jit(solution)/shard_map/ppermute | solution.py:21
  62.7 5.8 %collective-permute-start.13 = (f32[2,32,1]{1,2,0:T(1,128)S(1)}, f32[2,32,1]{1,2,0:T(1,128)S(1)}, u32[]{:S(2)}, u32[]{:S(2)}) collective-permute-start(f32[2,32,1]{1,2,0:T(1,128)S(1)} %get-tuple-element.26), channel_id=1, source_target_pairs={{1,0},{3,2},{5,4},{7,6},{9,8},{11,10},{13,12},{15,14},{17,16},{19,... | collective-permute-start | bytes 776 | tf_op jit(solution)/shard_map/ppermute | solution.py:23
  63.9 5.8 %collective-permute-start.14 = (f32[2,32,1]{1,2,0:T(1,128)S(1)}, f32[2,32,1]{1,2,0:T(1,128)S(1)}, u32[]{:S(2)}, u32[]{:S(2)}) collective-permute-start(f32[2,32,1]{1,2,0:T(1,128)S(1)} %get-tuple-element.27), channel_id=1, source_target_pairs={{0,1},{2,3},{4,5},{6,7},{8,9},{10,11},{12,13},{14,15},{16,17},{18,... | collective-permute-start | bytes 776 | tf_op jit(solution)/shard_map/ppermute | solution.py:21
  71.1 13.1 %collective-permute-start.15 = (f32[2,1,256]{1,2,0:T(8,128)S(1)}, f32[2,1,256]{1,2,0:T(8,128)S(1)}, u32[]{:S(2)}, u32[]{:S(2)}) collective-permute-start(f32[2,1,256]{1,2,0:T(8,128)S(1)} %get-tuple-element.20), channel_id=1, source_target_pairs={{2,0},{4,2},{6,4},{8,6},{10,8},{12,10},{14,12},{16,14},{18,16},{20... | collective-permute-start | bytes 6152 | tf_op jit(solution)/shard_map/ppermute | solution.py:23
  73.1 15.7 %collective-permute-start.16 = (f32[2,1,256]{1,2,0:T(8,128)S(1)}, f32[2,1,256]{1,2,0:T(8,128)S(1)}, u32[]{:S(2)}, u32[]{:S(2)}) collective-permute-start(f32[2,1,256]{1,2,0:T(8,128)S(1)} %get-tuple-element.21), channel_id=1, source_target_pairs={{0,2},{2,4},{4,6},{6,8},{8,10},{10,12},{12,14},{14,16},{16,18},{18... | collective-permute-start | bytes 6152 | tf_op jit(solution)/shard_map/ppermute | solution.py:21
  73.1 9.8 %collective-permute-start.17 = (f32[2,32,1]{1,2,0:T(1,128)S(1)}, f32[2,32,1]{1,2,0:T(1,128)S(1)}, u32[]{:S(2)}, u32[]{:S(2)}) collective-permute-start(f32[2,32,1]{1,2,0:T(1,128)S(1)} %get-tuple-element.22), channel_id=1, source_target_pairs={{1,0},{3,2},{5,4},{7,6},{9,8},{11,10},{13,12},{15,14},{17,16},{19,... | collective-permute-start | bytes 776 | tf_op jit(solution)/shard_map/ppermute | solution.py:23
  74.4 8.5 %collective-permute-start.18 = (f32[2,32,1]{1,2,0:T(1,128)S(1)}, f32[2,32,1]{1,2,0:T(1,128)S(1)}, u32[]{:S(2)}, u32[]{:S(2)}) collective-permute-start(f32[2,32,1]{1,2,0:T(1,128)S(1)} %get-tuple-element.23), channel_id=1, source_target_pairs={{0,1},{2,3},{4,5},{6,7},{8,9},{10,11},{12,13},{14,15},{16,17},{18,... | collective-permute-start | bytes 776 | tf_op jit(solution)/shard_map/ppermute | solution.py:21
  79.0 18.6 %collective-permute-start.19 = (f32[2,1,128]{2,1,0:T(1,128)S(1)}, f32[2,1,128]{2,1,0:T(1,128)S(1)}, u32[]{:S(2)}, u32[]{:S(2)}) collective-permute-start(f32[2,1,128]{2,1,0:T(1,128)S(1)} %broadcast.227), channel_id=1, source_target_pairs={{2,0},{4,2},{6,4},{8,6},{10,8},{12,10},{14,12},{16,14},{18,16},{20... | collective-permute-start | bytes 3080 | tf_op jit(solution)/shard_map/ppermute | solution.py:23
  82.9 14.6 %collective-permute-start.20 = (f32[2,1,128]{2,1,0:T(1,128)S(1)}, f32[2,1,128]{2,1,0:T(1,128)S(1)}, u32[]{:S(2)}, u32[]{:S(2)}) collective-permute-start(f32[2,1,128]{2,1,0:T(1,128)S(1)} %broadcast.227), channel_id=1, source_target_pairs={{0,2},{2,4},{4,6},{6,8},{8,10},{10,12},{12,14},{14,16},{16,18},{18... | collective-permute-start | bytes 3080 | tf_op jit(solution)/shard_map/ppermute | solution.py:21
  82.9 14.6 %collective-permute-start.21 = (f32[2,16,1]{2,1,0:T(8,128)S(1)}, f32[2,16,1]{2,1,0:T(8,128)S(1)}, u32[]{:S(2)}, u32[]{:S(2)}) collective-permute-start(f32[2,16,1]{2,1,0:T(8,128)S(1)} %broadcast.228), channel_id=1, source_target_pairs={{1,0},{3,2},{5,4},{7,6},{9,8},{11,10},{13,12},{15,14},{17,16},{19,... | collective-permute-start | bytes 392 | tf_op jit(solution)/shard_map/ppermute | solution.py:23
  84.2 13.3 %collective-permute-start.22 = (f32[2,16,1]{2,1,0:T(8,128)S(1)}, f32[2,16,1]{2,1,0:T(8,128)S(1)}, u32[]{:S(2)}, u32[]{:S(2)}) collective-permute-start(f32[2,16,1]{2,1,0:T(8,128)S(1)} %broadcast.228), channel_id=1, source_target_pairs={{0,1},{2,3},{4,5},{6,7},{8,9},{10,11},{12,13},{14,15},{16,17},{18,... | collective-permute-start | bytes 392 | tf_op jit(solution)/shard_map/ppermute | solution.py:21
  97.7 11.3 %collective-permute-start.23 = (f32[2,1,128]{2,1,0:T(1,128)S(1)}, f32[2,1,128]{2,1,0:T(1,128)S(1)}, u32[]{:S(2)}, u32[]{:S(2)}) collective-permute-start(f32[2,1,128]{2,1,0:T(1,128)S(1)} %get-tuple-element.42), channel_id=1, source_target_pairs={{2,0},{4,2},{6,4},{8,6},{10,8},{12,10},{14,12},{16,14},{18,16},{20... | collective-permute-start | bytes 3080 | tf_op jit(solution)/shard_map/ppermute | solution.py:23
  101.6 7.3 %collective-permute-start.24 = (f32[2,1,128]{2,1,0:T(1,128)S(1)}, f32[2,1,128]{2,1,0:T(1,128)S(1)}, u32[]{:S(2)}, u32[]{:S(2)}) collective-permute-start(f32[2,1,128]{2,1,0:T(1,128)S(1)} %get-tuple-element.43), channel_id=1, source_target_pairs={{0,2},{2,4},{4,6},{6,8},{8,10},{10,12},{12,14},{14,16},{16,18},{18... | collective-permute-start | bytes 3080 | tf_op jit(solution)/shard_map/ppermute | solution.py:21
  101.7 5.8 %collective-permute-start.25 = (f32[2,16,1]{2,1,0:T(8,128)S(1)}, f32[2,16,1]{2,1,0:T(8,128)S(1)}, u32[]{:S(2)}, u32[]{:S(2)}) collective-permute-start(f32[2,16,1]{2,1,0:T(8,128)S(1)} %get-tuple-element.44), channel_id=1, source_target_pairs={{1,0},{3,2},{5,4},{7,6},{9,8},{11,10},{13,12},{15,14},{17,16},{19,... | collective-permute-start | bytes 392 | tf_op jit(solution)/shard_map/ppermute | solution.py:23
  102.9 6.0 %collective-permute-start.26 = (f32[2,16,1]{2,1,0:T(8,128)S(1)}, f32[2,16,1]{2,1,0:T(8,128)S(1)}, u32[]{:S(2)}, u32[]{:S(2)}) collective-permute-start(f32[2,16,1]{2,1,0:T(8,128)S(1)} %get-tuple-element.45), channel_id=1, source_target_pairs={{0,1},{2,3},{4,5},{6,7},{8,9},{10,11},{12,13},{14,15},{16,17},{18,... | collective-permute-start | bytes 392 | tf_op jit(solution)/shard_map/ppermute | solution.py:21
  109.1 8.7 %collective-permute-start.29 = (f32[2,16,1]{2,1,0:T(8,128)S(1)}, f32[2,16,1]{2,1,0:T(8,128)S(1)}, u32[]{:S(2)}, u32[]{:S(2)}) collective-permute-start(f32[2,16,1]{2,1,0:T(8,128)S(1)} %get-tuple-element.40), channel_id=1, source_target_pairs={{1,0},{3,2},{5,4},{7,6},{9,8},{11,10},{13,12},{15,14},{17,16},{19,... | collective-permute-start | bytes 392 | tf_op jit(solution)/shard_map/ppermute | solution.py:23
  110.4 7.4 %collective-permute-start.30 = (f32[2,16,1]{2,1,0:T(8,128)S(1)}, f32[2,16,1]{2,1,0:T(8,128)S(1)}, u32[]{:S(2)}, u32[]{:S(2)}) collective-permute-start(f32[2,16,1]{2,1,0:T(8,128)S(1)} %get-tuple-element.41), channel_id=1, source_target_pairs={{0,1},{2,3},{4,5},{6,7},{8,9},{10,11},{12,13},{14,15},{16,17},{18,... | collective-permute-start | bytes 392 | tf_op jit(solution)/shard_map/ppermute | solution.py:21
  117.7 5.7 %collective-permute-start.28 = (f32[2,1,128]{2,1,0:T(1,128)S(1)}, f32[2,1,128]{2,1,0:T(1,128)S(1)}, u32[]{:S(2)}, u32[]{:S(2)}) collective-permute-start(f32[2,1,128]{2,1,0:T(1,128)S(1)} %get-tuple-element.39), channel_id=1, source_target_pairs={{0,2},{2,4},{4,6},{6,8},{8,10},{10,12},{12,14},{14,16},{16,18},{18... | collective-permute-start | bytes 3080 | tf_op jit(solution)/shard_map/ppermute | solution.py:21
  130.0 5.7 %collective-permute-start.32 = (f32[2,1,128]{2,1,0:T(1,128)S(1)}, f32[2,1,128]{2,1,0:T(1,128)S(1)}, u32[]{:S(2)}, u32[]{:S(2)}) collective-permute-start(f32[2,1,128]{2,1,0:T(1,128)S(1)} %get-tuple-element.51), channel_id=1, source_target_pairs={{0,2},{2,4},{4,6},{6,8},{8,10},{10,12},{12,14},{14,16},{16,18},{18... | collective-permute-start | bytes 3080 | tf_op jit(solution)/shard_map/ppermute | solution.py:21
  136.0 5.7 %collective-permute-start.34 = (f32[2,1,128]{2,1,0:T(1,128)S(1)}, f32[2,1,128]{2,1,0:T(1,128)S(1)}, u32[]{:S(2)}, u32[]{:S(2)}) collective-permute-start(f32[2,1,128]{2,1,0:T(1,128)S(1)} %get-tuple-element.49), channel_id=1, source_target_pairs={{0,2},{2,4},{4,6},{6,8},{8,10},{10,12},{12,14},{14,16},{16,18},{18... | collective-permute-start | bytes 3080 | tf_op jit(solution)/shard_map/ppermute | solution.py:21
  141.9 5.7 %collective-permute-start.36 = (f32[2,1,128]{2,1,0:T(1,128)S(1)}, f32[2,1,128]{2,1,0:T(1,128)S(1)}, u32[]{:S(2)}, u32[]{:S(2)}) collective-permute-start(f32[2,1,128]{2,1,0:T(1,128)S(1)} %get-tuple-element.47), channel_id=1, source_target_pairs={{0,2},{2,4},{4,6},{6,8},{8,10},{10,12},{12,14},{14,16},{16,18},{18... | collective-permute-start | bytes 3080 | tf_op jit(solution)/shard_map/ppermute | solution.py:21
  148.0 7.9 %collective-permute-start.37 = (f32[2,1,128]{2,1,0:T(1,128)S(1)}, f32[2,1,128]{2,1,0:T(1,128)S(1)}, u32[]{:S(2)}, u32[]{:S(2)}) collective-permute-start(f32[2,1,128]{2,1,0:T(1,128)S(1)} %get-tuple-element.34), channel_id=1, source_target_pairs={{2,0},{4,2},{6,4},{8,6},{10,8},{12,10},{14,12},{16,14},{18,16},{20... | collective-permute-start | bytes 3080 | tf_op jit(solution)/shard_map/ppermute | solution.py:23
  148.1 7.8 %collective-permute-start.38 = (f32[2,1,128]{2,1,0:T(1,128)S(1)}, f32[2,1,128]{2,1,0:T(1,128)S(1)}, u32[]{:S(2)}, u32[]{:S(2)}) collective-permute-start(f32[2,1,128]{2,1,0:T(1,128)S(1)} %get-tuple-element.35), channel_id=1, source_target_pairs={{0,2},{2,4},{4,6},{6,8},{8,10},{10,12},{12,14},{14,16},{16,18},{18... | collective-permute-start | bytes 3080 | tf_op jit(solution)/shard_map/ppermute | solution.py:21
  148.6 5.8 %collective-permute-start.39 = (f32[2,16,1]{2,1,0:T(8,128)S(1)}, f32[2,16,1]{2,1,0:T(8,128)S(1)}, u32[]{:S(2)}, u32[]{:S(2)}) collective-permute-start(f32[2,16,1]{2,1,0:T(8,128)S(1)} %get-tuple-element.36), channel_id=1, source_target_pairs={{1,0},{3,2},{5,4},{7,6},{9,8},{11,10},{13,12},{15,14},{17,16},{19,... | collective-permute-start | bytes 392 | tf_op jit(solution)/shard_map/ppermute | solution.py:23
  149.9 6.0 %collective-permute-start.40 = (f32[2,16,1]{2,1,0:T(8,128)S(1)}, f32[2,16,1]{2,1,0:T(8,128)S(1)}, u32[]{:S(2)}, u32[]{:S(2)}) collective-permute-start(f32[2,16,1]{2,1,0:T(8,128)S(1)} %get-tuple-element.37), channel_id=1, source_target_pairs={{0,1},{2,3},{4,5},{6,7},{8,9},{10,11},{12,13},{14,15},{16,17},{18,... | collective-permute-start | bytes 392 | tf_op jit(solution)/shard_map/ppermute | solution.py:21
  156.0 10.3 %collective-permute-start.41 = (f32[2,1,128]{2,1,0:T(1,128)S(1)}, f32[2,1,128]{2,1,0:T(1,128)S(1)}, u32[]{:S(2)}, u32[]{:S(2)}) collective-permute-start(f32[2,1,128]{2,1,0:T(1,128)S(1)} %get-tuple-element.30), channel_id=1, source_target_pairs={{2,0},{4,2},{6,4},{8,6},{10,8},{12,10},{14,12},{16,14},{18,16},{20... | collective-permute-start | bytes 3080 | tf_op jit(solution)/shard_map/ppermute | solution.py:23
  158.9 7.3 %collective-permute-start.42 = (f32[2,1,128]{2,1,0:T(1,128)S(1)}, f32[2,1,128]{2,1,0:T(1,128)S(1)}, u32[]{:S(2)}, u32[]{:S(2)}) collective-permute-start(f32[2,1,128]{2,1,0:T(1,128)S(1)} %get-tuple-element.31), channel_id=1, source_target_pairs={{0,2},{2,4},{4,6},{6,8},{8,10},{10,12},{12,14},{14,16},{16,18},{18... | collective-permute-start | bytes 3080 | tf_op jit(solution)/shard_map/ppermute | solution.py:21
  159.0 5.8 %collective-permute-start.43 = (f32[2,16,1]{2,1,0:T(8,128)S(1)}, f32[2,16,1]{2,1,0:T(8,128)S(1)}, u32[]{:S(2)}, u32[]{:S(2)}) collective-permute-start(f32[2,16,1]{2,1,0:T(8,128)S(1)} %get-tuple-element.32), channel_id=1, source_target_pairs={{1,0},{3,2},{5,4},{7,6},{9,8},{11,10},{13,12},{15,14},{17,16},{19,... | collective-permute-start | bytes 392 | tf_op jit(solution)/shard_map/ppermute | solution.py:23
  160.3 6.0 %collective-permute-start.44 = (f32[2,16,1]{2,1,0:T(8,128)S(1)}, f32[2,16,1]{2,1,0:T(8,128)S(1)}, u32[]{:S(2)}, u32[]{:S(2)}) collective-permute-start(f32[2,16,1]{2,1,0:T(8,128)S(1)} %get-tuple-element.33), channel_id=1, source_target_pairs={{0,1},{2,3},{4,5},{6,7},{8,9},{10,11},{12,13},{14,15},{16,17},{18,... | collective-permute-start | bytes 392 | tf_op jit(solution)/shard_map/ppermute | solution.py:21
  166.8 10.5 %collective-permute-start.45 = (f32[2,1,256]{1,2,0:T(8,128)S(1)}, f32[2,1,256]{1,2,0:T(8,128)S(1)}, u32[]{:S(2)}, u32[]{:S(2)}) collective-permute-start(f32[2,1,256]{1,2,0:T(8,128)S(1)} %get-tuple-element.16), channel_id=1, source_target_pairs={{2,0},{4,2},{6,4},{8,6},{10,8},{12,10},{14,12},{16,14},{18,16},{20... | collective-permute-start | bytes 6152 | tf_op jit(solution)/shard_map/ppermute | solution.py:23
  170.1 8.6 %collective-permute-start.46 = (f32[2,1,256]{1,2,0:T(8,128)S(1)}, f32[2,1,256]{1,2,0:T(8,128)S(1)}, u32[]{:S(2)}, u32[]{:S(2)}) collective-permute-start(f32[2,1,256]{1,2,0:T(8,128)S(1)} %get-tuple-element.17), channel_id=1, source_target_pairs={{0,2},{2,4},{4,6},{6,8},{8,10},{10,12},{12,14},{14,16},{16,18},{18... | collective-permute-start | bytes 6152 | tf_op jit(solution)/shard_map/ppermute | solution.py:21
  170.1 5.8 %collective-permute-start.47 = (f32[2,32,1]{1,2,0:T(1,128)S(1)}, f32[2,32,1]{1,2,0:T(1,128)S(1)}, u32[]{:S(2)}, u32[]{:S(2)}) collective-permute-start(f32[2,32,1]{1,2,0:T(1,128)S(1)} %get-tuple-element.18), channel_id=1, source_target_pairs={{1,0},{3,2},{5,4},{7,6},{9,8},{11,10},{13,12},{15,14},{17,16},{19,... | collective-permute-start | bytes 776 | tf_op jit(solution)/shard_map/ppermute | solution.py:23
  171.4 5.8 %collective-permute-start.48 = (f32[2,32,1]{1,2,0:T(1,128)S(1)}, f32[2,32,1]{1,2,0:T(1,128)S(1)}, u32[]{:S(2)}, u32[]{:S(2)}) collective-permute-start(f32[2,32,1]{1,2,0:T(1,128)S(1)} %get-tuple-element.19), channel_id=1, source_target_pairs={{0,1},{2,3},{4,5},{6,7},{8,9},{10,11},{12,13},{14,15},{16,17},{18,... | collective-permute-start | bytes 776 | tf_op jit(solution)/shard_map/ppermute | solution.py:21
  179.2 9.0 %collective-permute-start.49 = (f32[2,1,256]{1,2,0:T(8,128)S(1)}, f32[2,1,256]{1,2,0:T(8,128)S(1)}, u32[]{:S(2)}, u32[]{:S(2)}) collective-permute-start(f32[2,1,256]{1,2,0:T(8,128)S(1)} %get-tuple-element.12), channel_id=1, source_target_pairs={{2,0},{4,2},{6,4},{8,6},{10,8},{12,10},{14,12},{16,14},{18,16},{20... | collective-permute-start | bytes 6152 | tf_op jit(solution)/shard_map/ppermute | solution.py:23
  181.1 8.5 %collective-permute-start.50 = (f32[2,1,256]{1,2,0:T(8,128)S(1)}, f32[2,1,256]{1,2,0:T(8,128)S(1)}, u32[]{:S(2)}, u32[]{:S(2)}) collective-permute-start(f32[2,1,256]{1,2,0:T(8,128)S(1)} %get-tuple-element.13), channel_id=1, source_target_pairs={{0,2},{2,4},{4,6},{6,8},{8,10},{10,12},{12,14},{14,16},{16,18},{18... | collective-permute-start | bytes 6152 | tf_op jit(solution)/shard_map/ppermute | solution.py:21
  181.1 5.8 %collective-permute-start.51 = (f32[2,32,1]{1,2,0:T(1,128)S(1)}, f32[2,32,1]{1,2,0:T(1,128)S(1)}, u32[]{:S(2)}, u32[]{:S(2)}) collective-permute-start(f32[2,32,1]{1,2,0:T(1,128)S(1)} %get-tuple-element.14), channel_id=1, source_target_pairs={{1,0},{3,2},{5,4},{7,6},{9,8},{11,10},{13,12},{15,14},{17,16},{19,... | collective-permute-start | bytes 776 | tf_op jit(solution)/shard_map/ppermute | solution.py:23
  182.4 5.8 %collective-permute-start.52 = (f32[2,32,1]{1,2,0:T(1,128)S(1)}, f32[2,32,1]{1,2,0:T(1,128)S(1)}, u32[]{:S(2)}, u32[]{:S(2)}) collective-permute-start(f32[2,32,1]{1,2,0:T(1,128)S(1)} %get-tuple-element.15), channel_id=1, source_target_pairs={{0,1},{2,3},{4,5},{6,7},{8,9},{10,11},{12,13},{14,15},{16,17},{18,... | collective-permute-start | bytes 776 | tf_op jit(solution)/shard_map/ppermute | solution.py:21
  (6 other events, 14.4 us)
where the time goes:
time: 191 us
  starting transfers between devices  84 us (44%)
  waiting for transfers between devices  81.4 us (43%)
  local copies, waits for them, and re-layouts  10.7 us (6%)
  other arithmetic  8.63 us (5%)
  blocking collectives  4.93 us (3%)
    ppermute x24, starting transfers between devices, with_halo(): lax.ppermute(tail, axis, [(i, (i + 1) % count) for i in range(ends)])  49.2 us
    ppermute x5, waiting for transfers between devices, passed_along(): lax.ppermute(shard, axis, [(i, (i + by) % count) for i in range(count)])  40.3 us
    ppermute x24, waiting for transfers between devices, with_halo(): lax.ppermute(tail, axis, [(i, (i + 1) % count) for i in range(ends)])  34.3 us
    ppermute x24, starting transfers between devices, with_halo(): lax.ppermute(head, axis, [((i + 1) % count, i) for i in range(ends)])  34.1 us
    ppermute x24, waiting for transfers between devices, with_halo(): lax.ppermute(head, axis, [((i + 1) % count, i) for i in range(ends)])  6.86 us
    reshape x2, local copies, waits for them, and re-layouts, restrict(): return x.reshape(lev, nlon // 2, 2, nlat // 2, 2).mean(axis=(2, 4))  6.54 us
    all_gather x1, blocking collectives, per_device(): whole = lax.all_gather(rhs2, 'lat', axis=2, tiled=True)  4.93 us
  transfers between devices with their start and end apart: 53, of which 24 were waited for; matrix products, arithmetic and copies ran while one was open for 7% of the time, Pallas kernels for 0%

commit v1 on v0

v1 whole, which is shorter than its diff:
```python
import jax
import jax.numpy as jnp
from jax import lax
from jax.sharding import PartitionSpec as P

SMOOTH = 2
COARSE = 4
OMEGA = 0.8

LAT_HALO = 64
LON_HALO = 32


def pair_sum(x):
    zonal = jnp.roll(x, 1, axis=1) + jnp.roll(x, -1, axis=1)
    return zonal + jnp.roll(x, -1, axis=2) + jnp.roll(x, 1, axis=2)


def relax(x, rhs, coef, valid):
    diag = 1.0 + 4.0 * coef
    applied = diag * x - coef * pair_sum(x)
    x = x + OMEGA * (rhs - applied) / diag
    return jnp.where(valid, x, 0.0)


def defect(x, rhs, coef):
    diag = 1.0 + 4.0 * coef
    return rhs - (diag * x - coef * pair_sum(x))


def restrict(x):
    lev, nlon, nlat = x.shape
    return x.reshape(lev, nlon // 2, 2, nlat // 2, 2).mean(axis=(2, 4))


def prolong(x):
    return jnp.repeat(jnp.repeat(x, 2, axis=1), 2, axis=2)


def lat_rows_valid(first, count, nlat):
    rows = first + jnp.arange(count, dtype=jnp.int32)
    return ((rows >= 0) & (rows < nlat))[None, None, :]


def per_device(field, offsets, fraction, helm):
    lev, width, rows = field.shape
    n_lon = lax.axis_size("lon")
    n_lat = lax.axis_size("lat")
    nlon = width * n_lon
    nlat = rows * n_lat
    d = lax.axis_index("lon")
    l = lax.axis_index("lat")
    hh = LAT_HALO
    hl = LON_HALO

    pack = jnp.concatenate(
        [
            field.reshape(lev * width, rows),
            offsets.astype(jnp.float32)[None, :],
            fraction[None, :],
        ],
        axis=0,
    )
    below = lax.ppermute(pack[:, rows - hh :], "lat", [(i, i + 1) for i in range(n_lat - 1)])
    above = lax.ppermute(pack[:, :hh], "lat", [(i + 1, i) for i in range(n_lat - 1)])
    ext = jnp.concatenate([below, pack, above], axis=1)
    erows = rows + 2 * hh
    fld = ext[: lev * width].reshape(lev, width, erows)
    off_e = ext[lev * width].astype(jnp.int32)
    frac_e = ext[lev * width + 1]

    full = lax.all_gather(fld, "lon", axis=1, tiled=True)

    w0 = width + 2 * hl
    span = w0 + 16
    s0 = d * width - hl - 8
    amt = (off_e - s0) % nlon
    nbits = (nlon - 1).bit_length()
    top = 1 << (nbits - 1)
    take = (amt // top % 2 == 1)[None, None, :]
    y = jnp.where(take, jnp.roll(full, top, axis=1), full)
    need = top - 1
    y = jnp.concatenate([y[:, nlon - need :], y[:, :span]], axis=1) if need else y[:, :span]
    for bit in range(nbits - 2, -1, -1):
        b = 1 << bit
        take = (amt // b % 2 == 1)[None, None, :]
        lo = b
        y = jnp.where(take, y[:, : y.shape[1] - b], y[:, b:])
    win = y

    s = frac_e[None, None, :]
    w_one = -s * (s - 1.0) * (s - 2.0) / 6.0
    w_two = (s + 1.0) * (s - 1.0) * (s - 2.0) / 2.0
    w_three = -(s + 1.0) * s * (s - 2.0) / 2.0
    w_four = (s + 1.0) * s * (s - 1.0) / 6.0
    departure = (
        w_one * win[:, 9 : 9 + w0]
        + w_two * win[:, 8 : 8 + w0]
        + w_three * win[:, 7 : 7 + w0]
        + w_four * win[:, 6 : 6 + w0]
    )

    first = l * rows - hh
    valid0 = lat_rows_valid(first, erows, nlat)
    valid1 = lat_rows_valid(first // 2, erows // 2, nlat // 2)
    valid2 = lat_rows_valid(first // 4, erows // 4, nlat // 4)

    coef0 = helm[:, None, None]
    coef1 = coef0 / 4.0
    coef2 = coef0 / 16.0
    level0 = jnp.zeros_like(departure)
    for sweep in range(SMOOTH):
        level0 = relax(level0, departure, coef0, valid0)
    rhs1 = restrict(defect(level0, departure, coef0))
    level1 = jnp.zeros_like(rhs1)
    for sweep in range(SMOOTH):
        level1 = relax(level1, rhs1, coef1, valid1)
    rhs2 = restrict(defect(level1, rhs1, coef1))
    level2 = jnp.zeros_like(rhs2)
    for sweep in range(COARSE):
        level2 = relax(level2, rhs2, coef2, valid2)
    level1 = level1 + prolong(level2)
    for sweep in range(SMOOTH):
        level1 = relax(level1, rhs1, coef1, valid1)
    level0 = level0 + prolong(level1)
    for sweep in range(SMOOTH):
        level0 = relax(level0, departure, coef0, valid0)
    return level0[:, hl : hl + width, hh : hh + rows]


def solution(mesh):
    return jax.shard_map(
        per_device,
        mesh=mesh,
        in_specs=(P(None, "lon", "lat"), P("lat"), P("lat"), P()),
        out_specs=P(None, "lon", "lat"),
        check_vma=False,
    )
```

time: 191 us -> 132 us (0.69)
  starting transfers between devices: 84 us -> 6.16 us
  waiting for transfers between devices: 81.4 us -> 41.7 us
  local copies, waits for them, and re-layouts: 10.7 us -> 44.6 us
  other arithmetic: 8.63 us -> 25.4 us
  between operations: 0.79 us -> 14.1 us
  blocking collectives: 4.93 us -> 0 us
    ppermute x53 -> x2, starting transfers between devices: 84 us -> 6.16 us  [the longest x1 4.87 us: per_device(): lax.ppermute(pack[:, rows - hh:], 'lat', [(i, i + 1) for i in range(n_lat...]
    ppermute x53 -> x2, waiting for transfers between devices: 81.4 us -> 4.55 us  [the longest x1 4.24 us: per_device(): lax.ppermute(pack[:, :hh], 'lat', [(i + 1, i) for i in range(n_lat - 1)])]
    all_gather x0 -> x1, waiting for transfers between devices: none -> 37.1 us  [per_device(): full = lax.all_gather(fld, 'lon', axis=1, tiled=True)]
    reshape x2 -> x1, local copies, waits for them, and re-layouts: 6.54 us -> 20.5 us  [restrict(): return x.reshape(lev, nlon // 2, 2, nlat // 2, 2).mean(axis=(2, 4))]
    reduce_sum x2, other arithmetic: 3.01 us -> 15 us  [restrict(): return x.reshape(lev, nlon // 2, 2, nlat // 2, 2).mean(axis=(2, 4))]
    add x1 -> x2, local copies, waits for them, and re-layouts: 0.74 us -> 12.4 us  [pair_sum(): return zonal + jnp.roll(x, -1, axis=2) + jnp.roll(x, 1, axis=2)]
    div x1, local copies, waits for them, and re-layouts: 0.1 us -> 6.16 us  [restrict(): return x.reshape(lev, nlon // 2, 2, nlat // 2, 2).mean(axis=(2, 4))]
    all_gather x1 -> x0, blocking collectives: 4.93 us -> none  [per_device(): whole = lax.all_gather(rhs2, 'lat', axis=2, tiled=True)]
  transfers between devices with their start and end apart: 53 -> 3, of which waited for: 24 -> 3; matrix products, arithmetic and copies ran while one was open for 7% -> 2% of each run, Pallas kernels for 0% -> 0%
where the time goes in v1:
time: 132 us
  local copies, waits for them, and re-layouts  44.6 us (34%)
  waiting for transfers between devices  41.7 us (32%)
  other arithmetic  25.4 us (19%)
  between operations  14.1 us (11%)
  starting transfers between devices  6.16 us (5%)
    all_gather x1, waiting for transfers between devices, per_device(): full = lax.all_gather(fld, 'lon', axis=1, tiled=True)  37.1 us
    reshape x1, local copies, waits for them, and re-layouts, restrict(): return x.reshape(lev, nlon // 2, 2, nlat // 2, 2).mean(axis=(2, 4))  20.5 us
    reduce_sum x2, other arithmetic, restrict(): return x.reshape(lev, nlon // 2, 2, nlat // 2, 2).mean(axis=(2, 4))  15 us
    add x2, local copies, waits for them, and re-layouts, pair_sum(): return zonal + jnp.roll(x, -1, axis=2) + jnp.roll(x, 1, axis=2)  12.4 us
    div x1, local copies, waits for them, and re-layouts, restrict(): return x.reshape(lev, nlon // 2, 2, nlat // 2, 2).mean(axis=(2, 4))  6.16 us
    ppermute x1, starting transfers between devices, per_device(): lax.ppermute(pack[:, rows - hh:], 'lat', [(i, i + 1) for i in range(n_lat...  4.87 us
    ppermute x1, waiting for transfers between devices, per_device(): lax.ppermute(pack[:, :hh], 'lat', [(i + 1, i) for i in range(n_lat - 1)])  4.24 us
  transfers between devices with their start and end apart: 3, of which 3 were waited for; matrix products, arithmetic and copies ran while one was open for 2% of the time, Pallas kernels for 0%

profile of v1, /device:TPU:0, one launch (start us, length us, event | category | flops | bytes accessed | tf_op | source)
XLA Modules:
  0.0 131.9 jit_solution(12611783829817799280)
XLA Ops:
  6.5 0.7 convert_element_type.35
  7.2 0.9 pad_maximum_fusion.5
  8.2 4.9 %collective-permute-start = (f32[66,64]{1,0:T(8,128)S(1)}, f32[66,64]{1,0:T(8,128)S(1)}, u32[]{:S(2)}, u32[]{:S(2)}) collective-permute-start(f32[66,64]{1,0:T(8,128)S(1)} %get-tuple-element.83), channel_id=1, source_target_pairs={{0,1},{2,3},{4,5},{6,7},{8,9},{10,11},{12,13},{14,15},{16,17},{18,... | collective-permute-start | bytes 50696 | tf_op jit(solution)/shard_map/ppermute | solution.py:64
  13.0 1.3 collective-permute-start.1
  14.3 0.3 collective-permute-done
  14.6 4.2 %collective-permute-done.1 = f32[66,64]{1,0:T(8,128)S(1)} collective-permute-done((f32[66,64]{1,0:T(8,128)S(1)}, f32[66,64]{1,0:T(8,128)S(1)}, u32[]{:S(2)}, u32[]{:S(2)}) %collective-permute-start.1) | collective-permute-done | bytes 16928 | tf_op jit(solution)/shard_map/ppermute | solution.py:65
  18.9 1.6 %pad_maximum_fusion.1 = f32[64,384]{1,0:T(8,128)} fusion(f32[66,64]{1,0:T(8,128)S(1)} %collective-permute-done.1, f32[66,64]{1,0:T(8,128)S(1)} %collective-permute-done, f32[1,256]{1,0:T(1,128)} %bitcast.22, f32[1,256]{1,0:T(1,128)S(1)} %bitcast.18, f32[64,256]{1,0:T(8,128)} %bitcast.10), kind=kLoop, calls=%fused_computation.50 | loop fusion | flops 98304 | bytes 199680 | tf_op jit(solution)/shard_map/concatenate | solution.py:66
  20.7 0.1 copy.22
  20.8 0.1 concatenate.225
  20.9 0.1 concatenate.223
  21.2 0.7 broadcast_multiply_fusion.4
  21.8 0.8 maximum_reduce_fusion
  22.6 0.8 fusion.118
  23.5 37.1 %all-gather.2.cloned.1.call-done = f32[2,512,384]{2,1,0:T(8,128)} async-done(((f32[2,32,384]{2,1,0:T(8,128)}), f32[2,512,384]{2,1,0:T(8,128)}) %all-gather.2.cloned.1.call-update) | async-done | bytes 1572880 | tf_op jit(solution)/shard_map/all_gather | solution.py:72
  60.6 1.5 %fusion.123 = (f32[2,256,384]{2,1,0:T(8,128)S(1)}, f32[2,256,384]{2,1,0:T(8,128)S(1)}) fusion(f32[2,512,384]{2,1,0:T(8,128)} %all-gather.2.cloned.1.call-done), kind=kLoop, calls=%fused_computation.232 | loop fusion | bytes 3145728 | tf_op jit(solution)/shard_map/jit(_roll_static)/slice | solution.py:81
  62.1 1.6 %maximum_select_fusion = f32[2,512,384]{2,1,0:T(8,128)S(1)} fusion(f32[2,512,384]{2,1,0:T(8,128)} %all-gather.2.cloned.1.call-done, f32[2,256,384]{2,1,0:T(8,128)S(1)} %get-tuple-element.16, f32[2,256,384]{2,1,0:T(8,128)S(1)} %get-tuple-element.15, pred[384]{0:T(512)(128)(4,1)S(1)} %get-tuple-element.115), kind=kLoop, calls=%fused_computation.1 | loop fusion | flops 786432 | bytes 4718976 | tf_op jit(solution)/shard_map/jit(_where)/select_n | solution.py:81
  63.8 0.1 fusion
  64.3 0.3 copy-done
  64.6 0.2 divide_select_fusion
  64.8 0.1 fusion.138
  65.0 0.1 fusion.139
  65.1 0.3 fusion.29
  65.4 0.1 fusion.133
  65.7 0.2 fusion.16
  65.9 20.5 %reshape.406 = f32[2,48,2,192,2]{4,3,2,1,0:T(8,128)} reshape(f32[2,96,384]{2,1,0:T(8,128)S(1)} %fusion.16) | data formatting | bytes 589824 | tf_op jit(solution)/shard_map/reshape | solution.py:33
  86.4 8.1 %reduce_sum.18 = f32[2,48,192]{2,1,0:T(8,128)S(1)} reduce(f32[2,48,2,192,2]{4,3,2,1,0:T(8,128)} %reshape.406, f32[]{:T(128)} %constant.250.clone.1), dimensions={2,4}, to_apply=%region_0.1 | reduce | flops 55296 | bytes 368644 | tf_op jit(solution)/shard_map/reduce_sum | solution.py:33
  94.6 0.1 broadcast_multiply_fusion.1
  94.9 0.1 add_select_fusion
  95.2 0.1 fusion.33
  95.4 6.2 %add.488 = f32[2,24,2,96,2]{4,3,2,1,0:T(8,128)} reshape(f32[2,48,192]{2,1,0:T(8,128)S(1)} %fusion.33) | data formatting | bytes 147456 | tf_op jit(solution)/shard_map/add | solution.py:16
  101.6 6.2 %add.483 = f32[2,24,2,96,2]{4,3,2,1,0:T(8,128)} reshape(f32[2,48,192]{2,1,0:T(8,128)S(1)} %get-tuple-element.8) | data formatting | bytes 147456 | tf_op jit(solution)/shard_map/add | solution.py:16
  107.7 6.2 %div.246 = f32[2,24,2,96,2]{4,3,2,1,0:T(8,128)} reshape(f32[2,48,192]{2,1,0:T(8,128)S(1)} %get-tuple-element.73) | data formatting | bytes 147456 | tf_op jit(solution)/shard_map/div | solution.py:33
  113.9 6.9 %subtract_reduce_fusion = f32[2,24,96]{2,1,0:T(8,128)S(1)} fusion(f32[2,24,2,96,2]{4,3,2,1,0:T(8,128)} %div.246, f32[2,24,2,96,2]{4,3,2,1,0:T(8,128)} %add.488, f32[2,24,2,96,2]{4,3,2,1,0:T(8,128)} %add.483, f32[96,2]{1,0:T(8,128)S(1)} %concatenate.225, f32[24,2]{1,0:T(8,128)S(1)} %concatenate.223, f32[2]{0:T(128)S(1)} %get-tuple-element.127, ...), kind=kLoop, calls=%fused_computation | loop fusion | flops 364032 | bytes 240792 | tf_op jit(solution)/shard_map/reduce_sum | solution.py:33
  121.0 0.1 fusion.81
  121.3 0.1 fusion.80
  121.6 0.1 fusion.79
  121.9 0.1 copy.24
  122.2 0.1 fusion.51
  122.5 0.1 fusion.50
  122.8 0.1 copy.26
  123.0 0.1 broadcast_in_dim.207
  123.1 0.2 copy.27
  123.4 0.1 fusion.130
  123.5 0.1 fusion.131
  123.6 0.2 broadcast_multiply_fusion
  123.8 0.1 fusion.125
  124.1 0.2 fusion.27
  124.3 0.8 fusion.52
  (78 shorter events, 2.7 us)
Async XLA Ops:
  6.5 54.1 %all-gather.2.cloned.1.call-start = ((), (), s32[]{:S(2)}) async-start(), calls=%async_computation | async-start | bytes 1671168 | tf_op jit(solution)/shard_map/all_gather | solution.py:72
  8.2 6.5 %collective-permute-start = (f32[66,64]{1,0:T(8,128)S(1)}, f32[66,64]{1,0:T(8,128)S(1)}, u32[]{:S(2)}, u32[]{:S(2)}) collective-permute-start(f32[66,64]{1,0:T(8,128)S(1)} %get-tuple-element.83), channel_id=1, source_target_pairs={{0,1},{2,3},{4,5},{6,7},{8,9},{10,11},{12,13},{14,15},{16,17},{18,... | collective-permute-start | bytes 50696 | tf_op jit(solution)/shard_map/ppermute | solution.py:64
  13.0 5.9 %collective-permute-start.1 = (f32[66,64]{1,0:T(8,128)S(1)}, f32[66,64]{1,0:T(8,128)S(1)}, u32[]{:S(2)}, u32[]{:S(2)}) collective-permute-start(f32[66,64]{1,0:T(8,128)S(1)} %get-tuple-element.84), channel_id=1, source_target_pairs={{1,0},{3,2},{5,4},{7,6},{9,8},{11,10},{13,12},{15,14},{17,16},{19,... | collective-permute-start | bytes 50696 | tf_op jit(solution)/shard_map/ppermute | solution.py:65
  63.9 0.7 copy-start
Sparse Core Ops, SparseCore 0:
  20.6 39.9 all-gather.1

commit v2 on v1

v2 whole, which is shorter than its diff:
```python
import functools

import jax
import jax.numpy as jnp
from jax import lax
from jax.experimental import pallas as pl
from jax.experimental.pallas import tpu as pltpu
from jax.sharding import PartitionSpec as P

SMOOTH = 2
COARSE = 4
OMEGA = 0.8

LAT_HALO = 64
LON_HALO = 32


def vcycle_kernel(helm_ref, valid_ref, rhs_ref, out_ref, *, wlon):
    rows, cols = rhs_ref.shape
    b0 = rhs_ref[...]
    valid = valid_ref[...] > 0.5
    row = lax.broadcasted_iota(jnp.int32, (rows, cols), 0)
    col = lax.broadcasted_iota(jnp.int32, (rows, cols), 1)
    coef0 = jnp.where(row < wlon, helm_ref[0], helm_ref[1])

    def shift(x, by, axis):
        n = x.shape[axis]
        return pltpu.roll(x, by % n, axis)

    def pair_sum(x, step):
        zonal = shift(x, step, 0) + shift(x, -step, 0)
        return zonal + shift(x, -step, 1) + shift(x, step, 1)

    def relax(x, rhs, coef, diag, step):
        if x is None:
            x = OMEGA * rhs / diag
        else:
            applied = diag * x - coef * pair_sum(x, step)
            x = x + OMEGA * (rhs - applied) / diag
        return jnp.where(valid, x, 0.0)

    def defect(x, rhs, coef, diag, step):
        return rhs - (diag * x - coef * pair_sum(x, step))

    def restrict(x, step):
        lon_pair = x + shift(x, -step, 0)
        return (lon_pair + shift(lon_pair, -step, 1)) * 0.25

    def prolong(x, step):
        x = jnp.where(row % (2 * step) == step, shift(x, step, 0), x)
        return jnp.where(col % (2 * step) == step, shift(x, step, 1), x)

    coef1 = coef0 / 4.0
    coef2 = coef0 / 16.0
    diag0 = 1.0 + 4.0 * coef0
    diag1 = 1.0 + 4.0 * coef1
    diag2 = 1.0 + 4.0 * coef2

    x0 = None
    for sweep in range(SMOOTH):
        x0 = relax(x0, b0, coef0, diag0, 1)
    b1 = restrict(defect(x0, b0, coef0, diag0, 1), 1)
    x1 = None
    for sweep in range(SMOOTH):
        x1 = relax(x1, b1, coef1, diag1, 2)
    b2 = restrict(defect(x1, b1, coef1, diag1, 2), 2)
    x2 = None
    for sweep in range(COARSE):
        x2 = relax(x2, b2, coef2, diag2, 4)
    x1 = x1 + prolong(x2, 2)
    for sweep in range(SMOOTH):
        x1 = relax(x1, b1, coef1, diag1, 2)
    x0 = x0 + prolong(x1, 1)
    for sweep in range(SMOOTH):
        x0 = relax(x0, b0, coef0, diag0, 1)
    out_ref[...] = x0


def vcycle(helm, valid, rhs, wlon):
    return pl.pallas_call(
        functools.partial(vcycle_kernel, wlon=wlon),
        out_shape=jax.ShapeDtypeStruct(rhs.shape, rhs.dtype),
        in_specs=[
            pl.BlockSpec(memory_space=pltpu.SMEM),
            pl.BlockSpec(memory_space=pltpu.VMEM),
            pl.BlockSpec(memory_space=pltpu.VMEM),
        ],
        out_specs=pl.BlockSpec(memory_space=pltpu.VMEM),
        name="vcycle",
    )(helm, valid, rhs)


def per_device(field, offsets, fraction, helm):
    lev, width, rows = field.shape
    n_lon = lax.axis_size("lon")
    n_lat = lax.axis_size("lat")
    nlon = width * n_lon
    nlat = rows * n_lat
    d = lax.axis_index("lon")
    l = lax.axis_index("lat")
    hh = LAT_HALO
    hl = LON_HALO

    full = lax.all_gather(field, "lon", axis=1, tiled=True)

    w0 = width + 2 * hl
    span = w0 + 16
    s0 = d * width - hl - 8
    amt = (offsets - s0) % nlon
    nbits = (nlon - 1).bit_length()
    top = 1 << (nbits - 1)
    take = (amt // top % 2 == 1)[None, None, :]
    y = jnp.where(take, jnp.roll(full, top, axis=1), full)
    need = top - 1
    y = jnp.concatenate([y[:, nlon - need :], y[:, :span]], axis=1) if need else y[:, :span]
    for bit in range(nbits - 2, -1, -1):
        b = 1 << bit
        take = (amt // b % 2 == 1)[None, None, :]
        y = jnp.where(take, y[:, : y.shape[1] - b], y[:, b:])
    win = y

    s = fraction[None, None, :]
    w_one = -s * (s - 1.0) * (s - 2.0) / 6.0
    w_two = (s + 1.0) * (s - 1.0) * (s - 2.0) / 2.0
    w_three = -(s + 1.0) * s * (s - 2.0) / 2.0
    w_four = (s + 1.0) * s * (s - 1.0) / 6.0
    departure = (
        w_one * win[:, 9 : 9 + w0]
        + w_two * win[:, 8 : 8 + w0]
        + w_three * win[:, 7 : 7 + w0]
        + w_four * win[:, 6 : 6 + w0]
    )

    below = lax.ppermute(departure[:, :, rows - hh :], "lat", [(i, i + 1) for i in range(n_lat - 1)])
    above = lax.ppermute(departure[:, :, :hh], "lat", [(i + 1, i) for i in range(n_lat - 1)])
    ext = jnp.concatenate([below, departure, above], axis=2)
    erows = rows + 2 * hh

    first = l * rows - hh
    lat_rows = first + jnp.arange(erows, dtype=jnp.int32)
    valid = ((lat_rows >= 0) & (lat_rows < nlat)).astype(jnp.float32)[None, :]

    out = vcycle(helm, valid, ext.reshape(lev * w0, erows), w0)
    return out.reshape(lev, w0, erows)[:, hl : hl + width, hh : hh + rows]


def solution(mesh):
    return jax.shard_map(
        per_device,
        mesh=mesh,
        in_specs=(P(None, "lon", "lat"), P("lat"), P("lat"), P()),
        out_specs=P(None, "lon", "lat"),
        check_vma=False,
    )
```

time: 132 us -> 77 us (0.58)
  local copies, waits for them, and re-layouts: 44.6 us -> 4.58 us
  other arithmetic: 25.4 us -> 2.03 us
  Pallas kernels: 0 us -> 5.12 us
  waiting for transfers between devices: 41.7 us -> 46.8 us
  starting transfers between devices: 6.16 us -> 4.67 us
    reshape x5 -> x0, local copies, waits for them, and re-layouts: 21 us -> none  [the longest x1 20.5 us: restrict(): return x.reshape(lev, nlon // 2, 2, nlat // 2, 2).mean(axis=(2, 4))]
    reduce_sum x2 -> x0, other arithmetic: 15 us -> none  [restrict(): return x.reshape(lev, nlon // 2, 2, nlat // 2, 2).mean(axis=(2, 4))]
    add x2 -> x0, local copies, waits for them, and re-layouts: 12.4 us -> none  [pair_sum(): return zonal + jnp.roll(x, -1, axis=2) + jnp.roll(x, 1, axis=2)]
    div x1 -> x0, local copies, waits for them, and re-layouts: 6.16 us -> none  [restrict(): return x.reshape(lev, nlon // 2, 2, nlat // 2, 2).mean(axis=(2, 4))]
    pallas_call x0 -> x1, Pallas kernels: none -> 5.12 us  [vcycle(): pl.pallas_call(functools.partial(vcycle_kernel, wlon=wlon), out_shape=jax...]
    all_gather x1, waiting for transfers between devices: 37.1 us -> 41.5 us  [per_device(): full = lax.all_gather(field, 'lon', axis=1, tiled=True)]
    select_n x10 -> x0, other arithmetic: 2.09 us -> none  [relax(): return jnp.where(valid, x, 0.0)]
    concatenate x2 -> x1, other arithmetic: 2.45 us -> 0.89 us  [per_device(): ext = jnp.concatenate([below, departure, above], axis=2)]
  transfers between devices with their start and end apart: 3 -> 3, of which waited for: 3 -> 3; matrix products, arithmetic and copies ran while one was open for 2% -> 1% of each run, Pallas kernels for 0% -> 0%
where the time goes in v2:
time: 77 us; the launch traced here: 76.8 us
  waiting for transfers between devices  46.8 us (61%)
  between operations  13.5 us (18%)
  Pallas kernels  5.12 us (7%)
  starting transfers between devices  4.67 us (6%)
  local copies, waits for them, and re-layouts  4.58 us (6%)
  other arithmetic  2.03 us (3%)
    all_gather x1, waiting for transfers between devices, per_device(): full = lax.all_gather(field, 'lon', axis=1, tiled=True)  41.5 us
    pallas_call x1, Pallas kernels, vcycle(): pl.pallas_call(functools.partial(vcycle_kernel, wlon=wlon), out_shape=jax...  5.12 us
    ppermute x1, waiting for transfers between devices, per_device(): lax.ppermute(departure[:, :, :hh], 'lat', [(i + 1, i) for i in range(n_la...  4.12 us
    ppermute x1, starting transfers between devices, per_device(): lax.ppermute(departure[:, :, rows - hh:], 'lat', [(i, i + 1) for i in ran...  3.38 us
    slice x1, local copies, waits for them, and re-layouts, per_device(): return out.reshape(lev, w0, erows)[:, hl:hl + width, hh:hh + rows]  1.61 us
  transfers between devices with their start and end apart: 3, of which 3 were waited for; matrix products, arithmetic and copies ran while one was open for 1% of the time, Pallas kernels for 0%

profile of v2, /device:TPU:0, one launch (start us, length us, event | category | flops | bytes accessed | tf_op | source)
XLA Modules:
  0.0 76.8 jit_solution(5754602298189219821)
XLA Ops:
  6.5 0.0 all-gather.2.cloned.1.call-start
  6.5 0.7 all-gather.2.cloned.1.call-update
  7.3 0.0 copy-start.1
  7.3 0.7 copy-done.1
  8.0 0.0 copy-start.2
  8.0 0.6 copy-done.2
  8.7 41.5 %all-gather.2.cloned.1.call-done = f32[2,512,256]{2,1,0:T(8,128)} async-done(((f32[2,32,256]{2,1,0:T(8,128)}), f32[2,512,256]{2,1,0:T(8,128)}) %all-gather.2.cloned.1.call-update) | async-done | bytes 1048592 | tf_op jit(solution)/shard_map/all_gather | solution.py:104
  50.1 0.0 copy-start
  50.1 1.4 %fusion.29 = (f32[2,256,256]{2,1,0:T(8,128)S(1)}, f32[2,256,256]{2,1,0:T(8,128)S(1)}) fusion(f32[2,512,256]{2,1,0:T(8,128)} %all-gather.2.cloned.1.call-done), kind=kLoop, calls=%fused_computation.104 | loop fusion | bytes 2097152 | tf_op jit(solution)/shard_map/jit(_roll_static)/slice | solution.py:113
  51.5 0.2 copy-done
  51.7 0.1 maximum_select_fusion
  51.9 0.1 fusion
  52.2 0.1 fusion.1
  52.3 0.1 fusion.30
  52.4 3.4 %collective-permute-start = (f32[2,96,64]{2,1,0:T(8,128)S(1)}, f32[2,96,64]{2,1,0:T(8,128)S(1)}, u32[]{:S(2)}, u32[]{:S(2)}) collective-permute-start(f32[2,96,64]{2,1,0:T(8,128)S(1)} %get-tuple-element.11), channel_id=1, source_target_pairs={{0,1},{2,3},{4,5},{6,7},{8,9},{10,11},{12,13},{14,15},{16,17},{18,... | collective-permute-start | bytes 147464 | tf_op jit(solution)/shard_map/ppermute | solution.py:134
  55.8 1.3 %collective-permute-start.1 = (f32[2,96,64]{2,1,0:T(8,128)S(1)}, f32[2,96,64]{2,1,0:T(8,128)S(1)}, u32[]{:S(2)}, u32[]{:S(2)}) collective-permute-start(f32[2,96,64]{2,1,0:T(8,128)S(1)} %get-tuple-element.12), channel_id=1, source_target_pairs={{1,0},{3,2},{5,4},{7,6},{9,8},{11,10},{13,12},{15,14},{17,16},{19,... | collective-permute-start | bytes 147464 | tf_op jit(solution)/shard_map/ppermute | solution.py:135
  57.1 0.6 and_convert_fusion.valid_ref
  57.7 0.5 collective-permute-done
  58.2 4.1 %collective-permute-done.1 = f32[2,96,64]{2,1,0:T(8,128)S(1)} collective-permute-done((f32[2,96,64]{2,1,0:T(8,128)S(1)}, f32[2,96,64]{2,1,0:T(8,128)S(1)}, u32[]{:S(2)}, u32[]{:S(2)}) %collective-permute-start.1) | collective-permute-done | bytes 49184 | tf_op jit(solution)/shard_map/ppermute | solution.py:135
  62.3 0.9 %pad_maximum_fusion.1 = f32[2,96,384]{2,1,0:T(8,128)} fusion(f32[2,96,64]{2,1,0:T(8,128)S(1)} %collective-permute-done.1, f32[2,96,256]{2,1,0:T(8,128)S(1)} %fusion.1, f32[2,96,64]{2,1,0:T(8,128)S(1)} %collective-permute-done), kind=kLoop, calls=%fused_computation.5 | loop fusion | flops 147456 | bytes 589824 | tf_op jit(solution)/shard_map/concatenate | solution.py:136
  63.2 5.1 %vcycle.1 = f32[192,384]{1,0:T(8,128)} custom-call(f32[2]{0:T(128)} %helm_ref.1, f32[1,384]{1,0:T(1,128)} %and_convert_fusion.valid_ref, f32[192,384]{1,0:T(8,128)} %bitcast.2), custom_call_target="tpu_custom_call" | custom-call | tf_op jit(solution)/shard_map/vcycle/pallas_call | solution.py:80
  68.3 1.6 %slice.136 = f32[2,32,256]{2,1,0:T(8,128)} slice(f32[2,96,384]{2,1,0:T(8,128)} %bitcast.3), slice={[0:2], [32:64], [64:320]} | slice | bytes 131072 | tf_op jit(solution)/shard_map/slice | solution.py:144
  (13 shorter events, 0.3 us)
Async XLA Ops:
  6.5 43.6 %all-gather.2.cloned.1.call-start = ((), (), s32[]{:S(2)}) async-start(), calls=%async_computation | async-start | bytes 1114112 | tf_op jit(solution)/shard_map/all_gather | solution.py:104
  7.3 0.7 copy-start.1
  8.0 0.7 copy-start.2
  50.1 1.5 %copy-start = (f32[2,512,256]{2,1,0:T(8,128)S(1)}, f32[2,512,256]{2,1,0:T(8,128)}, u32[]{:S(2)}) copy-start(f32[2,512,256]{2,1,0:T(8,128)} %all-gather.2.cloned.1.call-done) | copy-start | bytes 3145732
  52.4 5.8 %collective-permute-start = (f32[2,96,64]{2,1,0:T(8,128)S(1)}, f32[2,96,64]{2,1,0:T(8,128)S(1)}, u32[]{:S(2)}, u32[]{:S(2)}) collective-permute-start(f32[2,96,64]{2,1,0:T(8,128)S(1)} %get-tuple-element.11), channel_id=1, source_target_pairs={{0,1},{2,3},{4,5},{6,7},{8,9},{10,11},{12,13},{14,15},{16,17},{18,... | collective-permute-start | bytes 147464 | tf_op jit(solution)/shard_map/ppermute | solution.py:134
  55.8 6.5 %collective-permute-start.1 = (f32[2,96,64]{2,1,0:T(8,128)S(1)}, f32[2,96,64]{2,1,0:T(8,128)S(1)}, u32[]{:S(2)}, u32[]{:S(2)}) collective-permute-start(f32[2,96,64]{2,1,0:T(8,128)S(1)} %get-tuple-element.12), channel_id=1, source_target_pairs={{1,0},{3,2},{5,4},{7,6},{9,8},{11,10},{13,12},{15,14},{17,16},{19,... | collective-permute-start | bytes 147464 | tf_op jit(solution)/shard_map/ppermute | solution.py:135
Sparse Core Ops, SparseCore 0:
  9.5 40.5 all-gather.1

commit v3 on v2

--- a/solution.py
+++ b/solution.py
@@ -96,17 +96,19 @@
     n_lat = lax.axis_size("lat")
     nlon = width * n_lon
     nlat = rows * n_lat
-    d = lax.axis_index("lon")
     l = lax.axis_index("lat")
     hh = LAT_HALO
     hl = LON_HALO
 
-    full = lax.all_gather(field, "lon", axis=1, tiled=True)
+    parts = [field] + [
+        lax.ppermute(field, "lon", [(i, (i - k) % n_lon) for i in range(n_lon)])
+        for k in range(1, n_lon)
+    ]
+    full = jnp.concatenate(parts, axis=1)
 
     w0 = width + 2 * hl
     span = w0 + 16
-    s0 = d * width - hl - 8
-    amt = (offsets - s0) % nlon
+    amt = (offsets + hl + 8) % nlon
     nbits = (nlon - 1).bit_length()
     top = 1 << (nbits - 1)
     take = (amt // top % 2 == 1)[None, None, :]

time: 77 us -> 55 us (0.71)
  waiting for transfers between devices: 46.8 us -> 15.9 us
  starting transfers between devices: 4.67 us -> 27.9 us
  between operations: 13.5 us -> 0.3 us
  local copies, waits for them, and re-layouts: 4.58 us -> 3.48 us
    all_gather x1 -> x0, waiting for transfers between devices: 41.5 us -> none  [per_device(): full = lax.all_gather(field, 'lon', axis=1, tiled=True)]
    ppermute x0 -> x15, starting transfers between devices: none -> 23.2 us  [per_device(): lax.ppermute(field, 'lon', [(i, (i - k) % n_lon) for i in range(n_lon)])]
    ppermute x0 -> x15, waiting for transfers between devices: none -> 11.2 us  [per_device(): lax.ppermute(field, 'lon', [(i, (i - k) % n_lon) for i in range(n_lon)])]
    slice x1 -> x0, local copies, waits for them, and re-layouts: 1.36 us -> none  [per_device(): y = jnp.where(take, jnp.roll(full, top, axis=1), full)]
    unnamed x6 -> x28, local copies, waits for them, and re-layouts: 1.47 us -> 1.72 us
  transfers between devices with their start and end apart: 3 -> 17, of which waited for: 3 -> 9; matrix products, arithmetic and copies ran while one was open for 1% -> 3% of each run, Pallas kernels for 0% -> 0%
where the time goes in v3:
time: 55 us; the launch traced here: 54.7 us
  starting transfers between devices  27.9 us (51%)
  waiting for transfers between devices  15.9 us (29%)
  Pallas kernels  5.13 us (9%)
  local copies, waits for them, and re-layouts  3.48 us (6%)
  other arithmetic  2.03 us (4%)
    ppermute x15, starting transfers between devices, per_device(): lax.ppermute(field, 'lon', [(i, (i - k) % n_lon) for i in range(n_lon)])  23.2 us
    ppermute x15, waiting for transfers between devices, per_device(): lax.ppermute(field, 'lon', [(i, (i - k) % n_lon) for i in range(n_lon)])  11.2 us
    pallas_call x1, Pallas kernels, vcycle(): pl.pallas_call(functools.partial(vcycle_kernel, wlon=wlon), out_shape=jax...  5.13 us
    ppermute x1, waiting for transfers between devices, per_device(): lax.ppermute(departure[:, :, :hh], 'lat', [(i + 1, i) for i in range(n_la...  4.32 us
    ppermute x1, starting transfers between devices, per_device(): lax.ppermute(departure[:, :, rows - hh:], 'lat', [(i, i + 1) for i in ran...  3.4 us
    unnamed x28, local copies, waits for them, and re-layouts  1.72 us
    slice x1, local copies, waits for them, and re-layouts, per_device(): return out.reshape(lev, w0, erows)[:, hl:hl + width, hh:hh + rows]  1.61 us
    ppermute x1, starting transfers between devices, per_device(): lax.ppermute(departure[:, :, :hh], 'lat', [(i + 1, i) for i in range(n_la...  1.29 us
  transfers between devices with their start and end apart: 17, of which 9 were waited for; matrix products, arithmetic and copies ran while one was open for 3% of the time, Pallas kernels for 0%

profile of v3, /device:TPU:0, one launch (start us, length us, event | category | flops | bytes accessed | tf_op | source)
XLA Modules:
  0.0 54.7 jit_solution(865069555538413692)
XLA Ops:
  0.0 0.0 copy-start.2
  0.0 5.5 %collective-permute-start.8 = (f32[2,32,256]{2,1,0:T(8,128)}, f32[2,32,256]{2,1,0:T(8,128)S(1)}, u32[]{:S(2)}, u32[]{:S(2)}) collective-permute-start(f32[2,32,256]{2,1,0:T(8,128)} %param.4), channel_id=1, source_target_pairs={{0,30},{2,0},{4,2},{6,4},{8,6},{10,8},{12,10},{14,12},{16,14},{18,... | collective-permute-start | bytes 196616 | tf_op jit(solution)/shard_map/ppermute | solution.py:104
  5.5 0.6 %collective-permute-start.9 = (f32[2,32,256]{2,1,0:T(8,128)}, f32[2,32,256]{2,1,0:T(8,128)S(1)}, u32[]{:S(2)}, u32[]{:S(2)}) collective-permute-start(f32[2,32,256]{2,1,0:T(8,128)} %param.4), channel_id=1, source_target_pairs={{0,28},{2,30},{4,0},{6,2},{8,4},{10,6},{12,8},{14,10},{16,12},{18,... | collective-permute-start | bytes 196616 | tf_op jit(solution)/shard_map/ppermute | solution.py:104
  6.1 0.2 collective-permute-start.10
  6.3 0.4 collective-permute-start.11
  6.8 0.1 collective-permute-start.12
  6.9 0.0 copy-done.2
  6.9 0.0 copy-start.1
  7.0 0.6 %copy-done.1 = f32[256]{0:T(256)S(1)} copy-done((f32[256]{0:T(256)S(1)}, f32[256]{0:T(256)}, u32[]{:S(2)}) %copy-start.1) | copy-done | bytes 1048
  7.6 0.9 %constant_dynamic-update-slice_fusion.31 = f32[2,512,256]{2,1,0:T(8,128)S(1)} fusion(f32[2,32,256]{2,1,0:T(8,128)} %param.4), kind=kLoop, calls=%fused_computation.49 | loop fusion | bytes 131072
  8.5 0.0 collective-permute-done.8
  8.5 0.0 copy-done
  8.5 4.4 %collective-permute-start.13 = (f32[2,32,256]{2,1,0:T(8,128)S(1)}, f32[2,32,256]{2,1,0:T(8,128)S(1)}, u32[]{:S(2)}, u32[]{:S(2)}) collective-permute-start(f32[2,32,256]{2,1,0:T(8,128)S(1)} %copy-done), channel_id=1, source_target_pairs={{0,20},{2,22},{4,24},{6,26},{8,28},{10,30},{12,0},{14,2},{16,4},{1... | collective-permute-start | bytes 196616 | tf_op jit(solution)/shard_map/ppermute | solution.py:104
  12.9 0.0 collective-permute-done.9
  12.9 0.1 collective-permute-start.14
  13.0 0.0 collective-permute-done.10
  13.0 1.6 %collective-permute-start = (f32[2,32,256]{2,1,0:T(8,128)S(1)}, f32[2,32,256]{2,1,0:T(8,128)S(1)}, u32[]{:S(2)}, u32[]{:S(2)}) collective-permute-start(f32[2,32,256]{2,1,0:T(8,128)S(1)} %copy-done), channel_id=1, source_target_pairs={{0,16},{2,18},{4,20},{6,22},{8,24},{10,26},{12,28},{14,30},{16,0},... | collective-permute-start | bytes 196616 | tf_op jit(solution)/shard_map/ppermute | solution.py:104
  14.7 0.0 collective-permute-done.11
  14.7 1.2 %collective-permute-start.1 = (f32[2,32,256]{2,1,0:T(8,128)S(1)}, f32[2,32,256]{2,1,0:T(8,128)S(1)}, u32[]{:S(2)}, u32[]{:S(2)}) collective-permute-start(f32[2,32,256]{2,1,0:T(8,128)S(1)} %copy-done), channel_id=1, source_target_pairs={{0,14},{2,16},{4,18},{6,20},{8,22},{10,24},{12,26},{14,28},{16,30}... | collective-permute-start | bytes 196616 | tf_op jit(solution)/shard_map/ppermute | solution.py:104
  15.8 0.0 collective-permute-done.12
  15.9 2.9 %collective-permute-start.2 = (f32[2,32,256]{2,1,0:T(8,128)S(1)}, f32[2,32,256]{2,1,0:T(8,128)S(1)}, u32[]{:S(2)}, u32[]{:S(2)}) collective-permute-start(f32[2,32,256]{2,1,0:T(8,128)S(1)} %copy-done), channel_id=1, source_target_pairs={{0,12},{2,14},{4,16},{6,18},{8,20},{10,22},{12,24},{14,26},{16,28}... | collective-permute-start | bytes 196616 | tf_op jit(solution)/shard_map/ppermute | solution.py:104
  18.8 0.0 collective-permute-done.13
  18.8 1.8 %collective-permute-start.3 = (f32[2,32,256]{2,1,0:T(8,128)S(1)}, f32[2,32,256]{2,1,0:T(8,128)S(1)}, u32[]{:S(2)}, u32[]{:S(2)}) collective-permute-start(f32[2,32,256]{2,1,0:T(8,128)S(1)} %copy-done), channel_id=1, source_target_pairs={{0,10},{2,12},{4,14},{6,16},{8,18},{10,20},{12,22},{14,24},{16,26}... | collective-permute-start | bytes 196616 | tf_op jit(solution)/shard_map/ppermute | solution.py:104
  20.6 0.0 collective-permute-done.14
  20.6 4.3 %collective-permute-start.4 = (f32[2,32,256]{2,1,0:T(8,128)S(1)}, f32[2,32,256]{2,1,0:T(8,128)S(1)}, u32[]{:S(2)}, u32[]{:S(2)}) collective-permute-start(f32[2,32,256]{2,1,0:T(8,128)S(1)} %copy-done), channel_id=1, source_target_pairs={{0,8},{2,10},{4,12},{6,14},{8,16},{10,18},{12,20},{14,22},{16,24},... | collective-permute-start | bytes 196616 | tf_op jit(solution)/shard_map/ppermute | solution.py:104
  24.9 2.8 %collective-permute-done = f32[2,32,256]{2,1,0:T(8,128)S(1)} collective-permute-done((f32[2,32,256]{2,1,0:T(8,128)S(1)}, f32[2,32,256]{2,1,0:T(8,128)S(1)}, u32[]{:S(2)}, u32[]{:S(2)}) %collective-permute-start) | collective-permute-done | bytes 65568 | tf_op jit(solution)/shard_map/ppermute | solution.py:104
  27.7 0.0 collective-permute-start.5
  27.8 0.9 %collective-permute-done.1 = f32[2,32,256]{2,1,0:T(8,128)S(1)} collective-permute-done((f32[2,32,256]{2,1,0:T(8,128)S(1)}, f32[2,32,256]{2,1,0:T(8,128)S(1)}, u32[]{:S(2)}, u32[]{:S(2)}) %collective-permute-start.1) | collective-permute-done | bytes 65568 | tf_op jit(solution)/shard_map/ppermute | solution.py:104
  28.7 0.0 collective-permute-start.6
  28.7 0.8 %collective-permute-done.2 = f32[2,32,256]{2,1,0:T(8,128)S(1)} collective-permute-done((f32[2,32,256]{2,1,0:T(8,128)S(1)}, f32[2,32,256]{2,1,0:T(8,128)S(1)}, u32[]{:S(2)}, u32[]{:S(2)}) %collective-permute-start.2) | collective-permute-done | bytes 65568 | tf_op jit(solution)/shard_map/ppermute | solution.py:104
  29.4 0.1 collective-permute-start.7
  29.6 0.8 %collective-permute-done.3 = f32[2,32,256]{2,1,0:T(8,128)S(1)} collective-permute-done((f32[2,32,256]{2,1,0:T(8,128)S(1)}, f32[2,32,256]{2,1,0:T(8,128)S(1)}, u32[]{:S(2)}, u32[]{:S(2)}) %collective-permute-start.3) | collective-permute-done | bytes 65568 | tf_op jit(solution)/shard_map/ppermute | solution.py:104
  30.4 0.0 collective-permute-done.4
  30.4 2.8 %collective-permute-done.5 = f32[2,32,256]{2,1,0:T(8,128)S(1)} collective-permute-done((f32[2,32,256]{2,1,0:T(8,128)S(1)}, f32[2,32,256]{2,1,0:T(8,128)S(1)}, u32[]{:S(2)}, u32[]{:S(2)}) %collective-permute-start.5) | collective-permute-done | bytes 65568 | tf_op jit(solution)/shard_map/ppermute | solution.py:104
  33.3 2.9 %collective-permute-done.6 = f32[2,32,256]{2,1,0:T(8,128)S(1)} collective-permute-done((f32[2,32,256]{2,1,0:T(8,128)S(1)}, f32[2,32,256]{2,1,0:T(8,128)S(1)}, u32[]{:S(2)}, u32[]{:S(2)}) %collective-permute-start.6) | collective-permute-done | bytes 65568 | tf_op jit(solution)/shard_map/ppermute | solution.py:104
  36.1 0.2 collective-permute-done.7
  36.5 0.1 broadcast_select_fusion
  36.7 0.1 fusion
  37.0 0.1 fusion.1
  37.1 0.1 fusion.29
  37.2 3.4 %collective-permute-start.15 = (f32[2,96,64]{2,1,0:T(8,128)S(1)}, f32[2,96,64]{2,1,0:T(8,128)S(1)}, u32[]{:S(2)}, u32[]{:S(2)}) collective-permute-start(f32[2,96,64]{2,1,0:T(8,128)S(1)} %get-tuple-element.9), channel_id=1, source_target_pairs={{0,1},{2,3},{4,5},{6,7},{8,9},{10,11},{12,13},{14,15},{16,17},{18,... | collective-permute-start | bytes 147464 | tf_op jit(solution)/shard_map/ppermute | solution.py:136
  40.6 1.3 %collective-permute-start.16 = (f32[2,96,64]{2,1,0:T(8,128)S(1)}, f32[2,96,64]{2,1,0:T(8,128)S(1)}, u32[]{:S(2)}, u32[]{:S(2)}) collective-permute-start(f32[2,96,64]{2,1,0:T(8,128)S(1)} %get-tuple-element.10), channel_id=1, source_target_pairs={{1,0},{3,2},{5,4},{7,6},{9,8},{11,10},{13,12},{15,14},{17,16},{19,... | collective-permute-start | bytes 147464 | tf_op jit(solution)/shard_map/ppermute | solution.py:137
  41.9 0.6 %and_convert_fusion.valid_ref = f32[1,384]{1,0:T(1,128)} fusion(s32[]{:T(128)S(6)} %sub.49), kind=kLoop, calls=%fused_computation.50 | loop fusion | flops 1920 | bytes 1540 | tf_op jit(solution)/shard_map/convert_element_type | solution.py:143
  42.5 0.3 collective-permute-done.15
  42.8 4.3 %collective-permute-done.16 = f32[2,96,64]{2,1,0:T(8,128)S(1)} collective-permute-done((f32[2,96,64]{2,1,0:T(8,128)S(1)}, f32[2,96,64]{2,1,0:T(8,128)S(1)}, u32[]{:S(2)}, u32[]{:S(2)}) %collective-permute-start.16) | collective-permute-done | bytes 49184 | tf_op jit(solution)/shard_map/ppermute | solution.py:137
  47.1 0.9 %pad_maximum_fusion.1 = f32[2,96,384]{2,1,0:T(8,128)} fusion(f32[2,96,64]{2,1,0:T(8,128)S(1)} %collective-permute-done.16, f32[2,96,256]{2,1,0:T(8,128)S(1)} %fusion.1, f32[2,96,64]{2,1,0:T(8,128)S(1)} %collective-permute-done.15), kind=kLoop, calls=%fused_computation.5 | loop fusion | flops 147456 | bytes 589824 | tf_op jit(solution)/shard_map/concatenate | solution.py:138
  48.0 5.1 %vcycle.1 = f32[192,384]{1,0:T(8,128)} custom-call(f32[2]{0:T(128)} %helm_ref.1, f32[1,384]{1,0:T(1,128)} %and_convert_fusion.valid_ref, f32[192,384]{1,0:T(8,128)} %bitcast.2), custom_call_target="tpu_custom_call" | custom-call | tf_op jit(solution)/shard_map/vcycle/pallas_call | solution.py:80
  53.1 1.6 %slice.130 = f32[2,32,256]{2,1,0:T(8,128)} slice(f32[2,96,384]{2,1,0:T(8,128)} %bitcast.3), slice={[0:2], [32:64], [64:320]} | slice | bytes 131072 | tf_op jit(solution)/shard_map/slice | solution.py:146
  (37 shorter events, 0.5 us)
Async XLA Ops:
  0.0 6.9 %copy-start.2 = (s32[256]{0:T(256)S(1)}, s32[256]{0:T(256)}, u32[]{:S(2)}) copy-start(s32[256]{0:T(256)} %param.5) | copy-start | bytes 3076
  0.0 8.5 %collective-permute-start.8 = (f32[2,32,256]{2,1,0:T(8,128)}, f32[2,32,256]{2,1,0:T(8,128)S(1)}, u32[]{:S(2)}, u32[]{:S(2)}) collective-permute-start(f32[2,32,256]{2,1,0:T(8,128)} %param.4), channel_id=1, source_target_pairs={{0,30},{2,0},{4,2},{6,4},{8,6},{10,8},{12,10},{14,12},{16,14},{18,... | collective-permute-start | bytes 196616 | tf_op jit(solution)/shard_map/ppermute | solution.py:104
  5.5 7.5 %collective-permute-start.9 = (f32[2,32,256]{2,1,0:T(8,128)}, f32[2,32,256]{2,1,0:T(8,128)S(1)}, u32[]{:S(2)}, u32[]{:S(2)}) collective-permute-start(f32[2,32,256]{2,1,0:T(8,128)} %param.4), channel_id=1, source_target_pairs={{0,28},{2,30},{4,0},{6,2},{8,4},{10,6},{12,8},{14,10},{16,12},{18,... | collective-permute-start | bytes 196616 | tf_op jit(solution)/shard_map/ppermute | solution.py:104
  6.1 6.9 %collective-permute-start.10 = (f32[2,32,256]{2,1,0:T(8,128)}, f32[2,32,256]{2,1,0:T(8,128)S(1)}, u32[]{:S(2)}, u32[]{:S(2)}) collective-permute-start(f32[2,32,256]{2,1,0:T(8,128)} %param.4), channel_id=1, source_target_pairs={{0,26},{2,28},{4,30},{6,0},{8,2},{10,4},{12,6},{14,8},{16,10},{18,... | collective-permute-start | bytes 196616 | tf_op jit(solution)/shard_map/ppermute | solution.py:104
  6.3 8.3 %collective-permute-start.11 = (f32[2,32,256]{2,1,0:T(8,128)}, f32[2,32,256]{2,1,0:T(8,128)S(1)}, u32[]{:S(2)}, u32[]{:S(2)}) collective-permute-start(f32[2,32,256]{2,1,0:T(8,128)} %param.4), channel_id=1, source_target_pairs={{0,24},{2,26},{4,28},{6,30},{8,0},{10,2},{12,4},{14,6},{16,8},{18,... | collective-permute-start | bytes 196616 | tf_op jit(solution)/shard_map/ppermute | solution.py:104
  6.8 9.1 %collective-permute-start.12 = (f32[2,32,256]{2,1,0:T(8,128)}, f32[2,32,256]{2,1,0:T(8,128)S(1)}, u32[]{:S(2)}, u32[]{:S(2)}) collective-permute-start(f32[2,32,256]{2,1,0:T(8,128)} %param.4), channel_id=1, source_target_pairs={{0,22},{2,24},{4,26},{6,28},{8,30},{10,0},{12,2},{14,4},{16,6},{18... | collective-permute-start | bytes 196616 | tf_op jit(solution)/shard_map/ppermute | solution.py:104
  6.9 0.7 %copy-start.1 = (f32[256]{0:T(256)S(1)}, f32[256]{0:T(256)}, u32[]{:S(2)}) copy-start(f32[256]{0:T(256)} %param.6) | copy-start | bytes 3076
  7.6 0.9 %copy-start = (f32[2,32,256]{2,1,0:T(8,128)S(1)}, f32[2,32,256]{2,1,0:T(8,128)}, u32[]{:S(2)}) copy-start(f32[2,32,256]{2,1,0:T(8,128)} %param.4) | copy-start | bytes 196612
  8.5 10.3 %collective-permute-start.13 = (f32[2,32,256]{2,1,0:T(8,128)S(1)}, f32[2,32,256]{2,1,0:T(8,128)S(1)}, u32[]{:S(2)}, u32[]{:S(2)}) collective-permute-start(f32[2,32,256]{2,1,0:T(8,128)S(1)} %copy-done), channel_id=1, source_target_pairs={{0,20},{2,22},{4,24},{6,26},{8,28},{10,30},{12,0},{14,2},{16,4},{1... | collective-permute-start | bytes 196616 | tf_op jit(solution)/shard_map/ppermute | solution.py:104
  12.9 7.7 %collective-permute-start.14 = (f32[2,32,256]{2,1,0:T(8,128)S(1)}, f32[2,32,256]{2,1,0:T(8,128)S(1)}, u32[]{:S(2)}, u32[]{:S(2)}) collective-permute-start(f32[2,32,256]{2,1,0:T(8,128)S(1)} %copy-done), channel_id=1, source_target_pairs={{0,18},{2,20},{4,22},{6,24},{8,26},{10,28},{12,30},{14,0},{16,2},{... | collective-permute-start | bytes 196616 | tf_op jit(solution)/shard_map/ppermute | solution.py:104
  13.0 14.7 %collective-permute-start = (f32[2,32,256]{2,1,0:T(8,128)S(1)}, f32[2,32,256]{2,1,0:T(8,128)S(1)}, u32[]{:S(2)}, u32[]{:S(2)}) collective-permute-start(f32[2,32,256]{2,1,0:T(8,128)S(1)} %copy-done), channel_id=1, source_target_pairs={{0,16},{2,18},{4,20},{6,22},{8,24},{10,26},{12,28},{14,30},{16,0},... | collective-permute-start | bytes 196616 | tf_op jit(solution)/shard_map/ppermute | solution.py:104
  14.7 14.0 %collective-permute-start.1 = (f32[2,32,256]{2,1,0:T(8,128)S(1)}, f32[2,32,256]{2,1,0:T(8,128)S(1)}, u32[]{:S(2)}, u32[]{:S(2)}) collective-permute-start(f32[2,32,256]{2,1,0:T(8,128)S(1)} %copy-done), channel_id=1, source_target_pairs={{0,14},{2,16},{4,18},{6,20},{8,22},{10,24},{12,26},{14,28},{16,30}... | collective-permute-start | bytes 196616 | tf_op jit(solution)/shard_map/ppermute | solution.py:104
  15.9 13.6 %collective-permute-start.2 = (f32[2,32,256]{2,1,0:T(8,128)S(1)}, f32[2,32,256]{2,1,0:T(8,128)S(1)}, u32[]{:S(2)}, u32[]{:S(2)}) collective-permute-start(f32[2,32,256]{2,1,0:T(8,128)S(1)} %copy-done), channel_id=1, source_target_pairs={{0,12},{2,14},{4,16},{6,18},{8,20},{10,22},{12,24},{14,26},{16,28}... | collective-permute-start | bytes 196616 | tf_op jit(solution)/shard_map/ppermute | solution.py:104
  18.8 11.6 %collective-permute-start.3 = (f32[2,32,256]{2,1,0:T(8,128)S(1)}, f32[2,32,256]{2,1,0:T(8,128)S(1)}, u32[]{:S(2)}, u32[]{:S(2)}) collective-permute-start(f32[2,32,256]{2,1,0:T(8,128)S(1)} %copy-done), channel_id=1, source_target_pairs={{0,10},{2,12},{4,14},{6,16},{8,18},{10,20},{12,22},{14,24},{16,26}... | collective-permute-start | bytes 196616 | tf_op jit(solution)/shard_map/ppermute | solution.py:104
  20.6 9.8 %collective-permute-start.4 = (f32[2,32,256]{2,1,0:T(8,128)S(1)}, f32[2,32,256]{2,1,0:T(8,128)S(1)}, u32[]{:S(2)}, u32[]{:S(2)}) collective-permute-start(f32[2,32,256]{2,1,0:T(8,128)S(1)} %copy-done), channel_id=1, source_target_pairs={{0,8},{2,10},{4,12},{6,14},{8,16},{10,18},{12,20},{14,22},{16,24},... | collective-permute-start | bytes 196616 | tf_op jit(solution)/shard_map/ppermute | solution.py:104
  27.7 5.5 %collective-permute-start.5 = (f32[2,32,256]{2,1,0:T(8,128)S(1)}, f32[2,32,256]{2,1,0:T(8,128)S(1)}, u32[]{:S(2)}, u32[]{:S(2)}) collective-permute-start(f32[2,32,256]{2,1,0:T(8,128)S(1)} %copy-done), channel_id=1, source_target_pairs={{0,6},{2,8},{4,10},{6,12},{8,14},{10,16},{12,18},{14,20},{16,22},{... | collective-permute-start | bytes 196616 | tf_op jit(solution)/shard_map/ppermute | solution.py:104
  28.7 7.5 %collective-permute-start.6 = (f32[2,32,256]{2,1,0:T(8,128)S(1)}, f32[2,32,256]{2,1,0:T(8,128)S(1)}, u32[]{:S(2)}, u32[]{:S(2)}) collective-permute-start(f32[2,32,256]{2,1,0:T(8,128)S(1)} %copy-done), channel_id=1, source_target_pairs={{0,4},{2,6},{4,8},{6,10},{8,12},{10,14},{12,16},{14,18},{16,20},{1... | collective-permute-start | bytes 196616 | tf_op jit(solution)/shard_map/ppermute | solution.py:104
  29.4 6.9 %collective-permute-start.7 = (f32[2,32,256]{2,1,0:T(8,128)S(1)}, f32[2,32,256]{2,1,0:T(8,128)S(1)}, u32[]{:S(2)}, u32[]{:S(2)}) collective-permute-start(f32[2,32,256]{2,1,0:T(8,128)S(1)} %copy-done), channel_id=1, source_target_pairs={{0,2},{2,4},{4,6},{6,8},{8,10},{10,12},{12,14},{14,16},{16,18},{18... | collective-permute-start | bytes 196616 | tf_op jit(solution)/shard_map/ppermute | solution.py:104
  37.2 5.6 %collective-permute-start.15 = (f32[2,96,64]{2,1,0:T(8,128)S(1)}, f32[2,96,64]{2,1,0:T(8,128)S(1)}, u32[]{:S(2)}, u32[]{:S(2)}) collective-permute-start(f32[2,96,64]{2,1,0:T(8,128)S(1)} %get-tuple-element.9), channel_id=1, source_target_pairs={{0,1},{2,3},{4,5},{6,7},{8,9},{10,11},{12,13},{14,15},{16,17},{18,... | collective-permute-start | bytes 147464 | tf_op jit(solution)/shard_map/ppermute | solution.py:136
  40.6 6.5 %collective-permute-start.16 = (f32[2,96,64]{2,1,0:T(8,128)S(1)}, f32[2,96,64]{2,1,0:T(8,128)S(1)}, u32[]{:S(2)}, u32[]{:S(2)}) collective-permute-start(f32[2,96,64]{2,1,0:T(8,128)S(1)} %get-tuple-element.10), channel_id=1, source_target_pairs={{1,0},{3,2},{5,4},{7,6},{9,8},{11,10},{13,12},{15,14},{17,16},{19,... | collective-permute-start | bytes 147464 | tf_op jit(solution)/shard_map/ppermute | solution.py:137
